TPU v7x, 256 devices: a whole 4x4x8 slice. The times are simulated.
256 devices in a mesh: expert: 128 (over x, z, y), hid: 2 (over core).
Axes of the slice: x: 4, y: 4, z: 8, core: 2. Of those that a mesh axis runs over, the one named last changes fastest.
Arguments:
- tokens: bfloat16 [16384, 3584], P('expert'), may hold values from -6 to 6
- out_grad: bfloat16 [16384, 3584], P('expert'), may hold values from -4 to 4
- route_ids: int32 [16384, 4], P('expert'), may hold values from 0 to 127, all different within a row; in each aligned block of 128 rows (0 to 127, 128 to 255, ...) at most 6 rows name the same one
- route_gates: float32 [16384, 4], P('expert'), may hold values from 0.1 to 1
- w_gate: bfloat16 [128, 3584, 1024], P('expert', None, 'hid'), may hold values from -0.09375 to 0.09375
- w_up: bfloat16 [128, 3584, 1024], P('expert', None, 'hid'), may hold values from -0.09375 to 0.09375
- w_down: bfloat16 [128, 1024, 3584], P('expert', 'hid'), may hold values from -0.1875 to 0.1875
Outputs:
- token_grad: bfloat16 [16384, 3584], P('expert', 'hid')
- gate_grad: bfloat16 [16384, 4], P('expert')
Inputs may be any that keep to these rules, and one draw needn't show every extreme that they name: `route_ids`: each token names 4 different experts. Among the 128 tokens of one index of expert (aligned blocks of rows), no expert is named more than 6 times, a bound that some block reaches.
All inputs are finite; a program needn't handle non-finite values.
Results may differ from a plain program's by a relative error of at most 0.008.
Values may be sent and summed in bfloat16 or wider, within the bound.
No kernel may reach another device: no remote copies, remote signals or barrier semaphores. Data moves between devices by JAX's collectives and lax.ppermute only.
A program may use at most 128 MiB of HBM per device.

v0:
```python
import jax
import jax.numpy as jnp
from jax import lax
from jax.sharding import PartitionSpec as P


def place_rows(source, dest_slot, slot_count):
    return jnp.zeros((slot_count, source.shape[1]), source.dtype).at[dest_slot].set(source)


def body(tokens, out_grad, route_ids, route_gates, w_gate, w_up, w_down):
    expert_count = lax.axis_size("expert")
    pair_count = lax.axis_size("hid")
    tok_rows, model_width = tokens.shape
    top_count = route_ids.shape[1]
    capacity = 3 * tok_rows * top_count // (2 * expert_count)
    slot_count = expert_count * capacity
    half_width = model_width // pair_count
    flat_ids = route_ids.reshape(-1)
    one_hot = (flat_ids[:, None] == jnp.arange(expert_count, dtype=jnp.int32)[None, :]).astype(
        jnp.int32
    )
    earlier = jnp.cumsum(one_hot, axis=0) - one_hot
    slot_index = jnp.sum(earlier * one_hot, axis=1)
    dest_slot = flat_ids * capacity + slot_index
    token_of = jnp.arange(tok_rows * top_count, dtype=jnp.int32) // top_count
    send_x = place_rows(tokens[token_of], dest_slot, slot_count).reshape(
        expert_count, capacity, model_width
    )
    send_d = place_rows(out_grad[token_of], dest_slot, slot_count).reshape(
        expert_count, capacity, model_width
    )
    rows_x, rows_d = (
        lax.all_to_all(send_x, "expert", split_axis=0, concat_axis=0, tiled=True),
        lax.all_to_all(send_d, "expert", split_axis=0, concat_axis=0, tiled=True),
    )
    rows_x = rows_x.reshape(slot_count, model_width)
    rows_d = rows_d.reshape(slot_count, model_width)
    gate_mat = w_gate[0]
    up_mat = w_up[0]
    down_mat = w_down[0]
    contract_last = (((1,), (1,)), ((), ()))
    gate_pre = jnp.dot(rows_x, gate_mat, preferred_element_type=jnp.float32)
    up_pre = jnp.dot(rows_x, up_mat, preferred_element_type=jnp.float32)
    grad_hidden = lax.dot_general(
        rows_d, down_mat, contract_last, preferred_element_type=jnp.float32
    )
    sigma_gate = jax.nn.sigmoid(gate_pre)
    act_gate = gate_pre * sigma_gate
    score_part = jnp.sum(act_gate * up_pre * grad_hidden, axis=1)
    grad_gate_pre = (
        grad_hidden * up_pre * sigma_gate * (1.0 + gate_pre * (1.0 - sigma_gate))
    ).astype(jnp.bfloat16)
    grad_up_pre = (grad_hidden * act_gate).astype(jnp.bfloat16)
    grad_part = lax.dot_general(
        grad_gate_pre, gate_mat, contract_last, preferred_element_type=jnp.float32
    ) + lax.dot_general(grad_up_pre, up_mat, contract_last, preferred_element_type=jnp.float32)
    grad_share = lax.psum_scatter(grad_part, "hid", scatter_dimension=1, tiled=True).astype(
        jnp.bfloat16
    )
    score_full = lax.psum(score_part, "hid").astype(jnp.bfloat16)
    back_grad, back_score = (
        lax.all_to_all(
            grad_share.reshape(expert_count, capacity, half_width),
            "expert",
            split_axis=0,
            concat_axis=0,
            tiled=True,
        ),
        lax.all_to_all(
            score_full.reshape(expert_count, capacity),
            "expert",
            split_axis=0,
            concat_axis=0,
            tiled=True,
        ),
    )
    picked = back_grad.reshape(slot_count, half_width)[dest_slot]
    picked = picked.reshape(tok_rows, top_count, half_width).astype(jnp.float32)
    token_grad = jnp.einsum("tkd,tk->td", picked, route_gates).astype(jnp.bfloat16)
    gate_grad = back_score.reshape(slot_count)[dest_slot].reshape(tok_rows, top_count)
    return (token_grad, gate_grad)


def solution(mesh):
    return jax.shard_map(
        body,
        mesh=mesh,
        in_specs=(
            P("expert", None),
            P("expert", None),
            P("expert", None),
            P("expert", None),
            P("expert", None, "hid"),
            P("expert", None, "hid"),
            P("expert", "hid", None),
        ),
        out_specs=(P("expert", "hid"), P("expert", None)),
        check_vma=False,
    )
```

profile of v0, /device:TPU:2, one launch (start us, length us, event | category | flops | bytes accessed | tf_op | source)
XLA Modules:
  0.0 563.0 jit_solution(16712479726074479944)
XLA Ops:
  9.9 19.8 %scatter_custom_fusion.1 = bf16[768,3584]{1,0:T(8,128)(2,1)} fusion(s32[512]{0:T(512)S(1)} %bitcast.45, bf16[128,3584]{1,0:T(8,128)(2,1)S(1)} %copy-done, s32[1024]{0:T(1024)S(1)} %pad_clamp_fusion.1, bf16[]{:T(256)} %constant.25.clone.1), kind=kCustom, calls=%fused_computation.16 | custom fusion | bytes 5505026 | tf_op jit(solution)/shard_map/scatter | solution.py:8
  29.6 9.6 %reshape.128 = bf16[128,6,3584]{2,1,0:T(8,128)(2,1)} reshape(bf16[768,3584]{1,0:T(8,128)(2,1)} %scatter_custom_fusion.1) | data formatting | bytes 11010048 | tf_op jit(solution)/shard_map/reshape | solution.py:27
  39.2 16.5 %all-to-all-start.1 = ((bf16[128,6,3584]{2,1,0:T(8,128)(2,1)}), bf16[128,6,3584]{2,1,0:T(8,128)(2,1)}, u32[]{:S(2)}, u32[]{:S(2)}) async-start(bf16[128,6,3584]{2,1,0:T(8,128)(2,1)} %reshape.128), calls=%async_computation.1 | async-start | bytes 14680064 | tf_op jit(solution)/shard_map/all_to_all | solution.py:34
  55.8 18.2 %scatter_custom_fusion = bf16[768,3584]{1,0:T(8,128)(2,1)} fusion(s32[512]{0:T(512)S(1)} %bitcast.46, bf16[128,3584]{1,0:T(8,128)(2,1)} %param.8, s32[1024]{0:T(1024)S(1)} %pad_clamp_fusion.1, bf16[]{:T(256)} %constant.25.clone.1), kind=kCustom, calls=%fused_computation.18 | custom fusion | bytes 5505536 | tf_op jit(solution)/shard_map/scatter | solution.py:8
  74.0 9.6 %reshape.126 = bf16[128,6,3584]{2,1,0:T(8,128)(2,1)} reshape(bf16[768,3584]{1,0:T(8,128)(2,1)} %scatter_custom_fusion) | data formatting | bytes 11010048 | tf_op jit(solution)/shard_map/reshape | solution.py:30
  83.6 136.7 %all-to-all-done.1 = bf16[128,6,3584]{2,1,0:T(8,128)(2,1)} async-done(((bf16[128,6,3584]{2,1,0:T(8,128)(2,1)}), bf16[128,6,3584]{2,1,0:T(8,128)(2,1)}, u32[]{:S(2)}, u32[]{:S(2)}) %all-to-all-start.1) | async-done | bytes 5505056 | tf_op jit(solution)/shard_map/all_to_all | solution.py:34
  220.2 7.8 %all-to-all-start = ((bf16[128,6,3584]{2,1,0:T(8,128)(2,1)}), bf16[128,6,3584]{2,1,0:T(8,128)(2,1)}, u32[]{:S(2)}, u32[]{:S(2)}) async-start(bf16[128,6,3584]{2,1,0:T(8,128)(2,1)} %reshape.126), calls=%async_computation | async-start | bytes 14680064 | tf_op jit(solution)/shard_map/all_to_all | solution.py:35
  228.1 9.9 %reshape.129 = bf16[768,3584]{1,0:T(8,128)(2,1)} reshape(bf16[128,6,3584]{2,1,0:T(8,128)(2,1)} %all-to-all-done.1) | data formatting | bytes 11010048 | tf_op jit(solution)/shard_map/reshape | solution.py:37
  238.0 6.9 %fusion.2 = f32[768,512]{0,1:T(8,128)S(1)} fusion(bf16[768,3584]{1,0:T(8,128)(2,1)} %reshape.129, bf16[1,3584,512]{2,1,0:T(8,128)(2,1)} %param.11), kind=kOutput, calls=%fused_computation.9 | convolution fusion | flops 2818572288 | bytes 10747904 | tf_op jit(solution)/shard_map/dot_general | solution.py:43
  244.9 3.1 fusion.5
  247.9 143.2 %all-to-all-done = bf16[128,6,3584]{2,1,0:T(8,128)(2,1)} async-done(((bf16[128,6,3584]{2,1,0:T(8,128)(2,1)}), bf16[128,6,3584]{2,1,0:T(8,128)(2,1)}, u32[]{:S(2)}, u32[]{:S(2)}) %all-to-all-start) | async-done | bytes 5505056 | tf_op jit(solution)/shard_map/all_to_all | solution.py:35
  391.1 9.7 %reshape.127 = bf16[768,3584]{1,0:T(8,128)(2,1)} reshape(bf16[128,6,3584]{2,1,0:T(8,128)(2,1)} %all-to-all-done) | data formatting | bytes 11010048 | tf_op jit(solution)/shard_map/reshape | solution.py:38
  400.8 7.0 %multiply_reduce_fusion = (f32[768]{0:T(1024)S(1)}, f32[768,512]{0,1:T(8,128)S(1)}) fusion(f32[768,512]{0,1:T(8,128)S(1)} %fusion.5, f32[768,512]{0,1:T(8,128)S(1)} %fusion.2, bf16[768,3584]{1,0:T(8,128)(2,1)} %reshape.127, bf16[1,512,3584]{2,1,0:T(8,128)(2,1)} %param.13), kind=kOutput, calls=%fused_computation.22 | convolution fusion | flops 2821324032 | bytes 13896704 | tf_op jit(solution)/shard_map/dot_general | solution.py:45
  407.8 3.6 fusion
  411.4 8.2 %convolution_add_fusion = f32[768,3584]{1,0:T(8,128)} fusion(f32[768,3584]{1,0:T(8,128)S(1)} %fusion, bf16[1,3584,512]{2,1,0:T(8,128)(2,1)} %param.12, f32[768,512]{0,1:T(8,128)S(1)} %get-tuple-element.7, f32[768,512]{0,1:T(8,128)S(1)} %fusion.2), kind=kOutput, calls=%fused_computation.6 | convolution fusion | flops 2823684096 | bytes 28835840 | tf_op jit(solution)/shard_map/dot_general | solution.py:57
  422.9 7.4 %all-to-all-start.3 = ((bf16[128,1,6]{2,1,0:T(2,128)(2,1)}), bf16[128,1,6]{2,1,0:T(2,128)(2,1)S(1)}, u32[]{:S(2)}, u32[]{:S(2)}) async-start(bf16[128,1,6]{2,1,0:T(2,128)(2,1)} %all_to_all.20), calls=%async_computation.4 | async-start | bytes 131072 | tf_op jit(solution)/shard_map/all_to_all | solution.py:70
  430.3 8.0 %reduce-scatter.2.cloned.1.call-done = f32[768,1792]{1,0:T(8,128)} async-done(((f32[768,3584]{1,0:T(8,128)}), f32[768,1792]{1,0:T(8,128)}) %reduce-scatter.2.cloned.1.call-update) | async-done | bytes 5505040 | tf_op jit(solution)/shard_map/reduce_scatter | solution.py:58
  438.3 2.8 convert_element_type.27
  443.8 14.4 %all-to-all-start.2 = ((bf16[128,6,1792]{2,1,0:T(8,128)(2,1)}), bf16[128,6,1792]{2,1,0:T(8,128)(2,1)}, u32[]{:S(2)}, u32[]{:S(2)}) async-start(bf16[128,6,1792]{2,1,0:T(8,128)(2,1)} %reshape.130), calls=%async_computation.3 | async-start | bytes 7340032 | tf_op jit(solution)/shard_map/all_to_all | solution.py:63
  458.7 3.5 gather_fusion.1
  463.0 80.4 %all-to-all-done.2 = bf16[128,6,1792]{2,1,0:T(8,128)(2,1)} async-done(((bf16[128,6,1792]{2,1,0:T(8,128)(2,1)}), bf16[128,6,1792]{2,1,0:T(8,128)(2,1)}, u32[]{:S(2)}, u32[]{:S(2)}) %all-to-all-start.2) | async-done | bytes 2752544 | tf_op jit(solution)/shard_map/all_to_all | solution.py:63
  543.5 4.0 reshape.131
  547.4 3.2 gather_fusion
  550.6 3.2 reshape.132
  (44 shorter events, 11.9 us)
Async XLA Ops:
  7.2 2.7 copy-start
  39.2 181.0 %all-to-all-start.1 = ((bf16[128,6,3584]{2,1,0:T(8,128)(2,1)}), bf16[128,6,3584]{2,1,0:T(8,128)(2,1)}, u32[]{:S(2)}, u32[]{:S(2)}) async-start(bf16[128,6,3584]{2,1,0:T(8,128)(2,1)} %reshape.128), calls=%async_computation.1 | async-start | bytes 14680064 | tf_op jit(solution)/shard_map/all_to_all | solution.py:34
  220.2 170.9 %all-to-all-start = ((bf16[128,6,3584]{2,1,0:T(8,128)(2,1)}), bf16[128,6,3584]{2,1,0:T(8,128)(2,1)}, u32[]{:S(2)}, u32[]{:S(2)}) async-start(bf16[128,6,3584]{2,1,0:T(8,128)(2,1)} %reshape.126), calls=%async_computation | async-start | bytes 14680064 | tf_op jit(solution)/shard_map/all_to_all | solution.py:35
  228.0 210.3 %reduce-scatter.2.cloned.1.call-start = ((), (), s32[]{:S(2)}) async-start(), calls=%async_computation.5 | async-start | bytes 16515072 | tf_op jit(solution)/shard_map/reduce_scatter | solution.py:58
  238.0 6.9 %copy-start.2 = (bf16[768,3584]{1,0:T(8,128)(2,1)S(1)}, bf16[768,3584]{1,0:T(8,128)(2,1)}, u32[]{:S(2)}) copy-start(bf16[768,3584]{1,0:T(8,128)(2,1)} %reshape.129) | copy-start | bytes 16515076
  238.0 6.9 %copy-start.4 = (bf16[1,3584,512]{2,1,0:T(8,128)(2,1)S(1)}, bf16[1,3584,512]{2,1,0:T(8,128)(2,1)}, u32[]{:S(2)}) copy-start(bf16[1,3584,512]{2,1,0:T(8,128)(2,1)} %param.12) | copy-start | bytes 11010052
  400.8 7.0 %copy-start.3 = (bf16[1,3584,512]{2,1,0:T(8,128)(2,1)S(1)}, bf16[1,3584,512]{2,1,0:T(8,128)(2,1)}, u32[]{:S(2)}) copy-start(bf16[1,3584,512]{2,1,0:T(8,128)(2,1)} %param.11) | copy-start | bytes 11010052
  422.9 20.9 %all-to-all-start.3 = ((bf16[128,1,6]{2,1,0:T(2,128)(2,1)}), bf16[128,1,6]{2,1,0:T(2,128)(2,1)S(1)}, u32[]{:S(2)}, u32[]{:S(2)}) async-start(bf16[128,1,6]{2,1,0:T(2,128)(2,1)} %all_to_all.20), calls=%async_computation.4 | async-start | bytes 131072 | tf_op jit(solution)/shard_map/all_to_all | solution.py:70
  443.8 14.4 %copy-start.5 = (f32[128,4]{0,1:T(4,128)S(1)}, f32[128,4]{0,1:T(4,128)}, u32[]{:S(2)}) copy-start(f32[128,4]{0,1:T(4,128)} %param.10) | copy-start | bytes 6148
  443.8 99.7 %all-to-all-start.2 = ((bf16[128,6,1792]{2,1,0:T(8,128)(2,1)}), bf16[128,6,1792]{2,1,0:T(8,128)(2,1)}, u32[]{:S(2)}, u32[]{:S(2)}) async-start(bf16[128,6,1792]{2,1,0:T(8,128)(2,1)} %reshape.130), calls=%async_computation.3 | async-start | bytes 7340032 | tf_op jit(solution)/shard_map/all_to_all | solution.py:63
  550.6 5.1 copy-start.1
Sparse Core Ops, SparseCore 0:
  419.7 18.5 reduce-scatter.1
where the time goes:
time: 573 us; the launch traced here: 563 us
  waiting for transfers between devices  368 us (64%)
  local copies, waits for them, and re-layouts  97.4 us (17%)
  starting transfers between devices  46.1 us (8%)
  matrix products  29.8 us (5%)
  between operations  14.7 us (3%)
    all_to_all x1, waiting for transfers between devices, body(): lax.all_to_all(send_d, 'expert', split_axis=0, concat_axis=0, tiled=True)  143 us
    all_to_all x1, waiting for transfers between devices, body(): lax.all_to_all(send_x, 'expert', split_axis=0, concat_axis=0, tiled=True)  137 us
    all_to_all x1, waiting for transfers between devices, body(): lax.all_to_all(grad_share.reshape(expert_count, capacity, half_width), 'e...  80.4 us
    scatter x2, local copies, waits for them, and re-layouts, place_rows(): jnp.zeros((slot_count, source.shape[1]), source.dtype).at[dest_slot]  38 us
    all_to_all x1, starting transfers between devices, body(): lax.all_to_all(send_x, 'expert', split_axis=0, concat_axis=0, tiled=True)  16.5 us
    all_to_all x1, starting transfers between devices, body(): lax.all_to_all(grad_share.reshape(expert_count, capacity, half_width), 'e...  14.4 us
  transfers between devices with their start and end apart: 5, of which 4 were waited for; matrix products, arithmetic and copies ran while one was open for 10% of the time, Pallas kernels for 0%

commit v1 on v0

--- a/solution.py
+++ b/solution.py
@@ -4,18 +4,16 @@
 from jax.sharding import PartitionSpec as P
 
 
-def place_rows(source, dest_slot, slot_count):
-    return jnp.zeros((slot_count, source.shape[1]), source.dtype).at[dest_slot].set(source)
-
-
 def body(tokens, out_grad, route_ids, route_gates, w_gate, w_up, w_down):
     expert_count = lax.axis_size("expert")
     pair_count = lax.axis_size("hid")
+    hid_idx = lax.axis_index("hid")
     tok_rows, model_width = tokens.shape
     top_count = route_ids.shape[1]
     capacity = 3 * tok_rows * top_count // (2 * expert_count)
     slot_count = expert_count * capacity
     half_width = model_width // pair_count
+    pair_total = tok_rows * top_count
     flat_ids = route_ids.reshape(-1)
     one_hot = (flat_ids[:, None] == jnp.arange(expert_count, dtype=jnp.int32)[None, :]).astype(
         jnp.int32
@@ -23,19 +21,19 @@
     earlier = jnp.cumsum(one_hot, axis=0) - one_hot
     slot_index = jnp.sum(earlier * one_hot, axis=1)
     dest_slot = flat_ids * capacity + slot_index
-    token_of = jnp.arange(tok_rows * top_count, dtype=jnp.int32) // top_count
-    send_x = place_rows(tokens[token_of], dest_slot, slot_count).reshape(
-        expert_count, capacity, model_width
+    slot_pair = jnp.zeros((slot_count,), jnp.int32).at[dest_slot].set(
+        jnp.arange(pair_total, dtype=jnp.int32)
     )
-    send_d = place_rows(out_grad[token_of], dest_slot, slot_count).reshape(
-        expert_count, capacity, model_width
+    slot_token = slot_pair // top_count
+    x_half = lax.dynamic_slice_in_dim(tokens, hid_idx * half_width, half_width, axis=1)
+    d_half = lax.dynamic_slice_in_dim(out_grad, hid_idx * half_width, half_width, axis=1)
+    send = jnp.stack([x_half[slot_token], d_half[slot_token]], axis=1).reshape(
+        expert_count, capacity, 2, half_width
     )
-    rows_x, rows_d = (
-        lax.all_to_all(send_x, "expert", split_axis=0, concat_axis=0, tiled=True),
-        lax.all_to_all(send_d, "expert", split_axis=0, concat_axis=0, tiled=True),
-    )
-    rows_x = rows_x.reshape(slot_count, model_width)
-    rows_d = rows_d.reshape(slot_count, model_width)
+    recv = lax.all_to_all(send, "expert", split_axis=0, concat_axis=0, tiled=True)
+    full = lax.all_gather(recv, "hid", axis=3, tiled=True)
+    rows_x = full[:, :, 0, :].reshape(slot_count, model_width)
+    rows_d = full[:, :, 1, :].reshape(slot_count, model_width)
     gate_mat = w_gate[0]
     up_mat = w_up[0]
     down_mat = w_down[0]

time: 573 us -> 490 us (0.86)
  waiting for transfers between devices: 368 us -> 112 us
  blocking collectives: 2.48 us -> 143 us
  local copies, waits for them, and re-layouts: 97.4 us -> 143 us
  starting transfers between devices: 46.1 us -> 28.8 us
    all_to_all x2 -> x0, waiting for transfers between devices: 280 us -> none  [the longest x1 143 us: body(): lax.all_to_all(send_d, 'expert', split_axis=0, concat_axis=0, tiled=True)]
    all_to_all x0 -> x1, blocking collectives: none -> 140 us  [body(): lax.all_to_all(send, 'expert', split_axis=0, concat_axis=0, tiled=True)]
    slice x0 -> x1, local copies, waits for them, and re-layouts: none -> 59.1 us  [body(): rows_d = full[:, :, 1, :].reshape(slot_count, model_width)]
    another operation x3 -> x8, local copies, waits for them, and re-layouts: 0.03 us -> 52.8 us  [the longest x3 33.3 us: body(): jnp.stack([x_half[slot_token], d_half[slot_token]], axis=1)]
    reshape x4 -> x0, local copies, waits for them, and re-layouts: 38.7 us -> none  [the longest x1 9.9 us: body(): rows_x = rows_x.reshape(slot_count, model_width)]
    scatter x2 -> x1, local copies, waits for them, and re-layouts: 38 us -> 2.45 us  [body(): jnp.zeros((slot_count,), jnp.int32).at[dest_slot]]
    all_to_all x2 -> x0, starting transfers between devices: 24.3 us -> none  [the longest x1 16.5 us: body(): lax.all_to_all(send_x, 'expert', split_axis=0, concat_axis=0, tiled=True)]
    all_gather x0 -> x1, waiting for transfers between devices: none -> 23.9 us  [body(): full = lax.all_gather(recv, 'hid', axis=3, tiled=True)]
  transfers between devices with their start and end apart: 5 -> 4, of which waited for: 4 -> 3; matrix products, arithmetic and copies ran while one was open for 10% -> 2% of each run, Pallas kernels for 0% -> 0%
where the time goes in v1:
time: 490 us; the launch traced here: 481 us
  local copies, waits for them, and re-layouts  143 us (29%)
  blocking collectives  143 us (29%)
  waiting for transfers between devices  112 us (23%)
  matrix products  29.5 us (6%)
  starting transfers between devices  28.8 us (6%)
  between operations  14.7 us (3%)
  other arithmetic  9.33 us (2%)
    all_to_all x1, blocking collectives, body(): lax.all_to_all(send, 'expert', split_axis=0, concat_axis=0, tiled=True)  140 us
    all_to_all x1, waiting for transfers between devices, body(): lax.all_to_all(grad_share.reshape(expert_count, capacity, half_width), 'e...  80.3 us
    slice x1, local copies, waits for them, and re-layouts, body(): rows_d = full[:, :, 1, :].reshape(slot_count, model_width)  59.1 us
    another operation x3, local copies, waits for them, and re-layouts, body(): jnp.stack([x_half[slot_token], d_half[slot_token]], axis=1)  33.3 us
    all_gather x1, waiting for transfers between devices, body(): full = lax.all_gather(recv, 'hid', axis=3, tiled=True)  23.9 us
    all_to_all x1, starting transfers between devices, body(): lax.all_to_all(grad_share.reshape(expert_count, capacity, half_width), 'e...  14.8 us
    all_to_all x1, starting transfers between devices, body(): lax.all_to_all(score_full.reshape(expert_count, capacity), 'expert', spli...  13.9 us
    another operation x1, local copies, waits for them, and re-layouts, body(): rows_d = full[:, :, 1, :].reshape(slot_count, model_width)  9.86 us
  transfers between devices with their start and end apart: 4, of which 3 were waited for; matrix products, arithmetic and copies ran while one was open for 2% of the time, Pallas kernels for 0%

profile of v1, /device:TPU:2, one launch (start us, length us, event | category | flops | bytes accessed | tf_op | source)
XLA Modules:
  0.0 480.6 jit_solution(7994707063346658145)
XLA Ops:
  13.5 4.1 gather_fusion
  17.6 5.4 %stack.9 = bf16[128,6,1,1792]{3,1,0,2:T(8,128)(2,1)} reshape(bf16[768,1792]{1,0:T(8,128)(2,1)} %gather_fusion) | data formatting | bytes 5505024 | tf_op jit(solution)/shard_map/stack | solution.py:30
  23.0 3.2 gather_fusion.1
  28.9 5.1 %pad_maximum_fusion = bf16[128,6,2,1792]{3,1,0,2:T(8,128)(2,1)S(1)} fusion(bf16[128,6,1,1792]{3,1,0,2:T(8,128)(2,1)} %stack.10, bf16[128,6,1,1792]{3,1,0,2:T(8,128)(2,1)} %stack.9), kind=kLoop, calls=%fused_computation.7 | loop fusion | flops 2752512 | bytes 11010048 | tf_op jit(solution)/shard_map/stack | solution.py:30
  34.1 25.1 %copy.20 = bf16[128,6,2,1792]{3,2,1,0:T(2,128)(2,1)S(1)} copy(bf16[128,6,2,1792]{3,1,0,2:T(8,128)(2,1)S(1)} %pad_maximum_fusion) | data formatting | bytes 11010048 | tf_op jit(solution)/shard_map/stack | solution.py:30
  59.2 140.2 %all_to_all.20 = bf16[128,6,2,1792]{3,2,1,0:T(2,128)(2,1)} all-to-all(bf16[128,6,2,1792]{3,2,1,0:T(2,128)(2,1)S(1)} %copy.20), channel_id=1, replica_groups=mesh['expert'=128,'hid'=2] {'expert'}, dimensions={0} | all-to-all | bytes 11010048 | tf_op jit(solution)/shard_map/all_to_all | solution.py:33
  199.5 23.9 %all-gather.2.cloned.1.call-done = bf16[128,6,2,3584]{3,2,1,0:T(2,128)(2,1)} async-done(((bf16[128,6,2,1792]{3,2,1,0:T(2,128)(2,1)}), bf16[128,6,2,3584]{3,2,1,0:T(2,128)(2,1)}) %all-gather.2.cloned.1.call-update) | async-done | bytes 11010064 | tf_op jit(solution)/shard_map/all_gather | solution.py:34
  223.4 59.1 %slice_reduce_fusion.1 = (bf16[128,6,3584]{2,1,0:T(8,128)(2,1)}, bf16[128,6,3584]{2,1,0:T(8,128)(2,1)}) fusion(bf16[128,6,2,3584]{3,2,1,0:T(2,128)(2,1)} %all-gather.2.cloned.1.call-done), kind=kLoop, calls=%fused_computation.6 | loop fusion | bytes 22020096 | tf_op jit(solution)/shard_map/slice | solution.py:36
  282.5 9.7 %reshape_squeeze.7 = bf16[768,3584]{1,0:T(8,128)(2,1)} reshape(bf16[128,6,3584]{2,1,0:T(8,128)(2,1)} %get-tuple-element.7) | data formatting | bytes 11010048 | tf_op jit(solution)/shard_map/reshape;squeeze | solution.py:35
  292.1 6.9 %fusion.2 = f32[768,512]{0,1:T(8,128)S(1)} fusion(bf16[768,3584]{1,0:T(8,128)(2,1)} %reshape_squeeze.7, bf16[1,3584,512]{2,1,0:T(8,128)(2,1)} %param.11), kind=kOutput, calls=%fused_computation.11 | convolution fusion | flops 2818572288 | bytes 10747904 | tf_op jit(solution)/shard_map/dot_general | solution.py:41
  299.0 3.1 fusion.5
  302.1 9.9 %reshape_squeeze.6 = bf16[768,3584]{1,0:T(8,128)(2,1)} reshape(bf16[128,6,3584]{2,1,0:T(8,128)(2,1)} %get-tuple-element.6) | data formatting | bytes 11010048 | tf_op jit(solution)/shard_map/reshape;squeeze | solution.py:36
  312.0 7.0 %multiply_reduce_fusion = (f32[768]{0:T(1024)S(1)}, f32[768,512]{0,1:T(8,128)S(1)}) fusion(f32[768,512]{0,1:T(8,128)S(1)} %fusion.5, f32[768,512]{0,1:T(8,128)S(1)} %fusion.2, bf16[768,3584]{1,0:T(8,128)(2,1)} %reshape_squeeze.6, bf16[1,512,3584]{2,1,0:T(8,128)(2,1)} %param.13), kind=kOutput, calls=%fused_computation.18 | convolution fusion | flops 2821324032 | bytes 13896704 | tf_op jit(solution)/shard_map/dot_general | solution.py:43
  318.9 3.6 fusion
  322.6 7.9 %convolution_add_fusion = f32[768,3584]{1,0:T(8,128)} fusion(f32[768,3584]{1,0:T(8,128)S(1)} %fusion, bf16[1,3584,512]{2,1,0:T(8,128)(2,1)} %param.12, f32[768,512]{0,1:T(8,128)S(1)} %get-tuple-element.9, f32[768,512]{0,1:T(8,128)S(1)} %fusion.2), kind=kOutput, calls=%fused_computation.8 | convolution fusion | flops 2823684096 | bytes 28835840 | tf_op jit(solution)/shard_map/dot_general | solution.py:55
  333.8 13.9 %all-to-all-start.2 = ((bf16[128,1,6]{2,1,0:T(2,128)(2,1)}), bf16[128,1,6]{2,1,0:T(2,128)(2,1)S(1)}, u32[]{:S(2)}, u32[]{:S(2)}) async-start(bf16[128,1,6]{2,1,0:T(2,128)(2,1)} %all_to_all.16), calls=%async_computation.3 | async-start | bytes 131072 | tf_op jit(solution)/shard_map/all_to_all | solution.py:68
  347.7 8.0 %reduce-scatter.2.cloned.1.call-done = f32[768,1792]{1,0:T(8,128)} async-done(((f32[768,3584]{1,0:T(8,128)}), f32[768,1792]{1,0:T(8,128)}) %reduce-scatter.2.cloned.1.call-update) | async-done | bytes 5505040 | tf_op jit(solution)/shard_map/reduce_scatter | solution.py:56
  355.7 2.8 convert_element_type.27
  361.2 14.8 %all-to-all-start.1 = ((bf16[128,6,1792]{2,1,0:T(8,128)(2,1)}), bf16[128,6,1792]{2,1,0:T(8,128)(2,1)}, u32[]{:S(2)}, u32[]{:S(2)}) async-start(bf16[128,6,1792]{2,1,0:T(8,128)(2,1)} %reshape.76), calls=%async_computation.2 | async-start | bytes 7340032 | tf_op jit(solution)/shard_map/all_to_all | solution.py:61
  376.6 3.5 gather_fusion.3
  380.9 80.3 %all-to-all-done.1 = bf16[128,6,1792]{2,1,0:T(8,128)(2,1)} async-done(((bf16[128,6,1792]{2,1,0:T(8,128)(2,1)}), bf16[128,6,1792]{2,1,0:T(8,128)(2,1)}, u32[]{:S(2)}, u32[]{:S(2)}) %all-to-all-start.1) | async-done | bytes 2752544 | tf_op jit(solution)/shard_map/all_to_all | solution.py:61
  461.2 4.0 reshape.77
  465.1 3.2 gather_fusion.2
  468.3 3.1 reshape.78
  (46 shorter events, 18.2 us)
Async XLA Ops:
  7.2 216.2 %all-gather.2.cloned.1.call-start = ((), (), s32[]{:S(2)}) async-start(), calls=%async_computation.4 | async-start | bytes 16515072 | tf_op jit(solution)/shard_map/all_gather | solution.py:34
  199.5 156.2 %reduce-scatter.2.cloned.1.call-start = ((), (), s32[]{:S(2)}) async-start(), calls=%async_computation.5 | async-start | bytes 16515072 | tf_op jit(solution)/shard_map/reduce_scatter | solution.py:56
  292.1 6.9 %copy-start = (bf16[768,3584]{1,0:T(8,128)(2,1)S(1)}, bf16[768,3584]{1,0:T(8,128)(2,1)}, u32[]{:S(2)}) copy-start(bf16[768,3584]{1,0:T(8,128)(2,1)} %reshape_squeeze.7) | copy-start | bytes 16515076
  292.1 6.9 %copy-start.2 = (bf16[1,3584,512]{2,1,0:T(8,128)(2,1)S(1)}, bf16[1,3584,512]{2,1,0:T(8,128)(2,1)}, u32[]{:S(2)}) copy-start(bf16[1,3584,512]{2,1,0:T(8,128)(2,1)} %param.12) | copy-start | bytes 11010052
  312.0 7.0 %copy-start.1 = (bf16[1,3584,512]{2,1,0:T(8,128)(2,1)S(1)}, bf16[1,3584,512]{2,1,0:T(8,128)(2,1)}, u32[]{:S(2)}) copy-start(bf16[1,3584,512]{2,1,0:T(8,128)(2,1)} %param.11) | copy-start | bytes 11010052
  333.8 27.4 %all-to-all-start.2 = ((bf16[128,1,6]{2,1,0:T(2,128)(2,1)}), bf16[128,1,6]{2,1,0:T(2,128)(2,1)S(1)}, u32[]{:S(2)}, u32[]{:S(2)}) async-start(bf16[128,1,6]{2,1,0:T(2,128)(2,1)} %all_to_all.16), calls=%async_computation.3 | async-start | bytes 131072 | tf_op jit(solution)/shard_map/all_to_all | solution.py:68
  361.2 14.9 %copy-start.3 = (f32[128,4]{0,1:T(4,128)S(1)}, f32[128,4]{0,1:T(4,128)}, u32[]{:S(2)}) copy-start(f32[128,4]{0,1:T(4,128)} %param.10) | copy-start | bytes 6148
  361.2 99.9 %all-to-all-start.1 = ((bf16[128,6,1792]{2,1,0:T(8,128)(2,1)}), bf16[128,6,1792]{2,1,0:T(8,128)(2,1)}, u32[]{:S(2)}, u32[]{:S(2)}) async-start(bf16[128,6,1792]{2,1,0:T(8,128)(2,1)} %reshape.76), calls=%async_computation.2 | async-start | bytes 7340032 | tf_op jit(solution)/shard_map/all_to_all | solution.py:61
Sparse Core Ops, SparseCore 0:
  199.6 23.7 all-gather.1
  330.7 24.9 reduce-scatter.1

commit v2 on v1

--- a/solution.py
+++ b/solution.py
@@ -25,15 +25,12 @@
         jnp.arange(pair_total, dtype=jnp.int32)
     )
     slot_token = slot_pair // top_count
-    x_half = lax.dynamic_slice_in_dim(tokens, hid_idx * half_width, half_width, axis=1)
-    d_half = lax.dynamic_slice_in_dim(out_grad, hid_idx * half_width, half_width, axis=1)
-    send = jnp.stack([x_half[slot_token], d_half[slot_token]], axis=1).reshape(
-        expert_count, capacity, 2, half_width
-    )
+    source = jnp.where(hid_idx == 0, tokens, out_grad)
+    send = source[slot_token].reshape(expert_count, capacity // 2, 2, model_width)
     recv = lax.all_to_all(send, "expert", split_axis=0, concat_axis=0, tiled=True)
-    full = lax.all_gather(recv, "hid", axis=3, tiled=True)
-    rows_x = full[:, :, 0, :].reshape(slot_count, model_width)
-    rows_d = full[:, :, 1, :].reshape(slot_count, model_width)
+    both = lax.all_gather(recv, "hid", axis=0, tiled=False)
+    rows_x = both[0].reshape(slot_count, model_width)
+    rows_d = both[1].reshape(slot_count, model_width)
     gate_mat = w_gate[0]
     up_mat = w_up[0]
     down_mat = w_down[0]
@@ -57,26 +54,22 @@
         jnp.bfloat16
     )
     score_full = lax.psum(score_part, "hid").astype(jnp.bfloat16)
-    back_grad, back_score = (
-        lax.all_to_all(
-            grad_share.reshape(expert_count, capacity, half_width),
-            "expert",
-            split_axis=0,
-            concat_axis=0,
-            tiled=True,
-        ),
-        lax.all_to_all(
-            score_full.reshape(expert_count, capacity),
-            "expert",
-            split_axis=0,
-            concat_axis=0,
-            tiled=True,
-        ),
-    )
-    picked = back_grad.reshape(slot_count, half_width)[dest_slot]
-    picked = picked.reshape(tok_rows, top_count, half_width).astype(jnp.float32)
-    token_grad = jnp.einsum("tkd,tk->td", picked, route_gates).astype(jnp.bfloat16)
-    gate_grad = back_score.reshape(slot_count)[dest_slot].reshape(tok_rows, top_count)
+    score_cols = jnp.zeros((slot_count, 128), jnp.bfloat16).at[:, 0].set(score_full)
+    back_send = jnp.concatenate([grad_share, score_cols], axis=1)
+    back_width = back_send.shape[1]
+    back = lax.all_to_all(
+        back_send.reshape(expert_count, capacity // 2, 2, back_width),
+        "expert",
+        split_axis=0,
+        concat_axis=0,
+        tiled=True,
+    ).reshape(slot_count, back_width)
+    picked = back[dest_slot]
+    pair_grad = picked[:, :half_width].reshape(tok_rows, top_count, half_width)
+    token_grad = jnp.einsum(
+        "tkd,tk->td", pair_grad.astype(jnp.float32), route_gates
+    ).astype(jnp.bfloat16)
+    gate_grad = picked[:, half_width].reshape(tok_rows, top_count)
     return (token_grad, gate_grad)
 
 

time: 490 us -> 399 us (0.81); the launches traced: 481 us -> 397 us
  local copies, waits for them, and re-layouts: 143 us -> 72.8 us
  starting transfers between devices: 28.8 us -> 14.7 us
    slice x1 -> x3, local copies, waits for them, and re-layouts: 59.1 us -> 13.2 us  [the longest x1 10.6 us: body(): rows_x = both[0].reshape(slot_count, model_width)]
    another operation x8 -> x7, local copies, waits for them, and re-layouts: 52.8 us -> 24 us  [the longest x1 11.9 us: body(): rows_d = both[1].reshape(slot_count, model_width)]
    all_to_all x2 -> x1, starting transfers between devices: 28.7 us -> 14.4 us  [body(): lax.all_to_all(back_send.reshape(expert_count, capacity // 2, 2, back_wid...]
    reduce_scatter x1, waiting for transfers between devices: 8 us -> 21.2 us  [body(): lax.psum_scatter(grad_part, 'hid', scatter_dimension=1, tiled=True)]
    reshape x5 -> x4, local copies, waits for them, and re-layouts: 10 us -> 21.5 us  [the longest x1 11.4 us: body(): source[slot_token].reshape(expert_count, capacity // 2, 2, model_width)]
    all_to_all x2 -> x1, waiting for transfers between devices: 80.3 us -> 70 us  [body(): lax.all_to_all(back_send.reshape(expert_count, capacity // 2, 2, back_wid...]
    gather x4 -> x2, local copies, waits for them, and re-layouts: 14 us -> 8.66 us  [the longest x1 5.45 us: body(): source[slot_token].reshape(expert_count, capacity // 2, 2, model_width)]
  transfers between devices with their start and end apart: 4 -> 3, of which waited for: 3 -> 3; matrix products, arithmetic and copies ran while one was open for 2% -> 0% of each run, Pallas kernels for 0% -> 0%
where the time goes in v2:
time: 399 us; the launch traced here: 397 us
  blocking collectives  143 us (36%)
  waiting for transfers between devices  115 us (29%)
  local copies, waits for them, and re-layouts  72.8 us (18%)
  matrix products  31 us (8%)
  starting transfers between devices  14.7 us (4%)
  between operations  14.3 us (4%)
  other arithmetic  6.83 us (2%)
    all_to_all x1, blocking collectives, body(): lax.all_to_all(send, 'expert', split_axis=0, concat_axis=0, tiled=True)  140 us
    all_to_all x1, waiting for transfers between devices, body(): lax.all_to_all(back_send.reshape(expert_count, capacity // 2, 2, back_wid...  70 us
    all_gather x1, waiting for transfers between devices, body(): both = lax.all_gather(recv, 'hid', axis=0, tiled=False)  23.7 us
    reduce_scatter x1, waiting for transfers between devices, body(): lax.psum_scatter(grad_part, 'hid', scatter_dimension=1, tiled=True)  21.2 us
    all_to_all x1, starting transfers between devices, body(): lax.all_to_all(back_send.reshape(expert_count, capacity // 2, 2, back_wid...  14.4 us
    another operation x1, local copies, waits for them, and re-layouts, body(): rows_d = both[1].reshape(slot_count, model_width)  11.9 us
    another operation x1, local copies, waits for them, and re-layouts, body(): rows_x = both[0].reshape(slot_count, model_width)  11.8 us
    reshape x1, local copies, waits for them, and re-layouts, body(): source[slot_token].reshape(expert_count, capacity // 2, 2, model_width)  11.4 us
  transfers between devices with their start and end apart: 3, of which 3 were waited for; matrix products, arithmetic and copies ran while one was open for 0% of the time, Pallas kernels for 0%

profile of v2, /device:TPU:2, one launch (start us, length us, event | category | flops | bytes accessed | tf_op | source)
XLA Modules:
  0.0 397.4 jit_solution(14922912729927147166)
XLA Ops:
  9.8 2.4 scatter_custom_fusion
  13.6 5.5 %gather_fusion = bf16[768,3584]{1,0:T(8,128)(2,1)} fusion(bf16[128,3584]{1,0:T(8,128)(2,1)S(1)} %broadcast_select_fusion, s32[1024]{0:T(1024)S(1)} %pad_clamp_fusion.1), kind=kCustom, calls=%fused_computation | custom fusion | bytes 11013120 | tf_op jit(solution)/shard_map/gather | solution.py:29
  19.0 11.4 %reshape.91 = bf16[128,3,2,3584]{3,2,1,0:T(2,128)(2,1)} reshape(bf16[768,3584]{1,0:T(8,128)(2,1)} %gather_fusion) | data formatting | bytes 11010048 | tf_op jit(solution)/shard_map/reshape | solution.py:29
  30.4 140.4 %all_to_all.10 = bf16[128,3,2,3584]{3,2,1,0:T(2,128)(2,1)} all-to-all(bf16[128,3,2,3584]{3,2,1,0:T(2,128)(2,1)} %reshape.91), channel_id=1, replica_groups=mesh['expert'=128,'hid'=2] {'expert'}, dimensions={0} | all-to-all | bytes 11010048 | tf_op jit(solution)/shard_map/all_to_all | solution.py:30
  171.1 23.7 %all-gather.3.cloned.1.call-done = bf16[256,3,2,3584]{3,2,1,0:T(2,128)(2,1)} async-done(((bf16[128,3,2,3584]{3,2,1,0:T(2,128)(2,1)}), bf16[256,3,2,3584]{3,2,1,0:T(2,128)(2,1)}) %all-gather.3.cloned.1.call-update) | async-done | bytes 11010064 | tf_op jit(solution)/shard_map/all_gather | solution.py:31
  194.8 10.6 %fusion.25 = (bf16[128,3,2,3584]{3,2,1,0:T(2,128)(2,1)}, bf16[128,3,2,3584]{3,2,1,0:T(2,128)(2,1)}) fusion(bf16[256,3,2,3584]{3,2,1,0:T(2,128)(2,1)} %all-gather.3.cloned.1.call-done), kind=kLoop, calls=%fused_computation.53 | loop fusion | bytes 22020096 | tf_op jit(solution)/shard_map/slice | solution.py:32
  205.4 11.8 %reshape_squeeze.10 = bf16[768,3584]{1,0:T(8,128)(2,1)} reshape(bf16[128,3,2,3584]{3,2,1,0:T(2,128)(2,1)} %get-tuple-element.20) | data formatting | bytes 11010048 | tf_op jit(solution)/shard_map/reshape;squeeze | solution.py:32
  217.3 6.9 %fusion.3 = f32[768,512]{0,1:T(8,128)S(1)} fusion(bf16[768,3584]{1,0:T(8,128)(2,1)} %reshape_squeeze.10, bf16[1,3584,512]{2,1,0:T(8,128)(2,1)} %param.13), kind=kOutput, calls=%fused_computation.8 | convolution fusion | flops 2818572288 | bytes 10747904 | tf_op jit(solution)/shard_map/dot_general | solution.py:38
  224.2 3.1 fusion.6
  227.2 11.9 %reshape_squeeze.9 = bf16[768,3584]{1,0:T(8,128)(2,1)} reshape(bf16[128,3,2,3584]{3,2,1,0:T(2,128)(2,1)} %get-tuple-element.21) | data formatting | bytes 11010048 | tf_op jit(solution)/shard_map/reshape;squeeze | solution.py:33
  239.1 7.0 %multiply_reduce_fusion = (f32[768]{0:T(1024)S(1)}, f32[768,512]{0,1:T(8,128)S(1)}) fusion(f32[768,512]{0,1:T(8,128)S(1)} %fusion.6, f32[768,512]{0,1:T(8,128)S(1)} %fusion.3, bf16[768,3584]{1,0:T(8,128)(2,1)} %reshape_squeeze.9, bf16[1,512,3584]{2,1,0:T(8,128)(2,1)} %param.15), kind=kOutput, calls=%fused_computation.16 | convolution fusion | flops 2821324032 | bytes 13896704 | tf_op jit(solution)/shard_map/dot_general | solution.py:40
  246.1 3.6 fusion.1
  249.7 7.9 %convolution_add_fusion = f32[768,3584]{1,0:T(8,128)} fusion(f32[768,3584]{1,0:T(8,128)S(1)} %fusion.1, bf16[1,3584,512]{2,1,0:T(8,128)(2,1)} %param.14, f32[768,512]{0,1:T(8,128)S(1)} %get-tuple-element.23, f32[768,512]{0,1:T(8,128)S(1)} %fusion.3), kind=kOutput, calls=%fused_computation.3 | convolution fusion | flops 2823684096 | bytes 28835840 | tf_op jit(solution)/shard_map/dot_general | solution.py:52
  258.3 2.4 psum.7
  261.6 21.2 %reduce-scatter.2.cloned.1.call-done = f32[768,1792]{1,0:T(8,128)} async-done(((f32[768,3584]{1,0:T(8,128)}), f32[768,1792]{1,0:T(8,128)}) %reduce-scatter.2.cloned.1.call-update) | async-done | bytes 5505040 | tf_op jit(solution)/shard_map/reduce_scatter | solution.py:53
  282.8 2.8 convert_element_type.27
  285.9 2.6 reshape.93
  288.5 14.4 %all-to-all-start.1 = ((bf16[128,3,2,1920]{3,2,1,0:T(2,128)(2,1)}), bf16[128,3,2,1920]{3,2,1,0:T(2,128)(2,1)}, u32[]{:S(2)}, u32[]{:S(2)}) async-start(bf16[128,3,2,1920]{3,2,1,0:T(2,128)(2,1)} %reshape.93), calls=%async_computation.2 | async-start | bytes 5898240 | tf_op jit(solution)/shard_map/all_to_all | solution.py:60
  303.1 70.0 %all-to-all-done.1 = bf16[128,3,2,1920]{3,2,1,0:T(2,128)(2,1)} async-done(((bf16[128,3,2,1920]{3,2,1,0:T(2,128)(2,1)}), bf16[128,3,2,1920]{3,2,1,0:T(2,128)(2,1)}, u32[]{:S(2)}, u32[]{:S(2)}) %all-to-all-start.1) | async-done | bytes 2949152 | tf_op jit(solution)/shard_map/all_to_all | solution.py:60
  373.1 6.0 %reshape.94 = bf16[768,1920]{1,0:T(8,128)(2,1)S(1)} reshape(bf16[128,3,2,1920]{3,2,1,0:T(2,128)(2,1)} %all-to-all-done.1) | data formatting | bytes 5898240 | tf_op jit(solution)/shard_map/reshape | solution.py:66
  379.1 3.2 gather_fusion.1
  382.3 1.6 slice.47
  384.9 1.5 reshape.95
  386.4 2.6 fusion.26
  (42 shorter events, 8.6 us)
Async XLA Ops:
  7.2 187.7 %all-gather.3.cloned.1.call-start = ((), (), s32[]{:S(2)}) async-start(), calls=%async_computation.4 | async-start | bytes 16515072 | tf_op jit(solution)/shard_map/all_gather | solution.py:31
  170.9 111.9 %reduce-scatter.2.cloned.1.call-start = ((), (), s32[]{:S(2)}) async-start(), calls=%async_computation.3 | async-start | bytes 16515072 | tf_op jit(solution)/shard_map/reduce_scatter | solution.py:53
  217.3 6.9 %copy-start = (bf16[768,3584]{1,0:T(8,128)(2,1)S(1)}, bf16[768,3584]{1,0:T(8,128)(2,1)}, u32[]{:S(2)}) copy-start(bf16[768,3584]{1,0:T(8,128)(2,1)} %reshape_squeeze.10) | copy-start | bytes 16515076
  217.3 6.9 %copy-start.2 = (bf16[1,3584,512]{2,1,0:T(8,128)(2,1)S(1)}, bf16[1,3584,512]{2,1,0:T(8,128)(2,1)}, u32[]{:S(2)}) copy-start(bf16[1,3584,512]{2,1,0:T(8,128)(2,1)} %param.14) | copy-start | bytes 11010052
  239.1 7.0 %copy-start.1 = (bf16[1,3584,512]{2,1,0:T(8,128)(2,1)S(1)}, bf16[1,3584,512]{2,1,0:T(8,128)(2,1)}, u32[]{:S(2)}) copy-start(bf16[1,3584,512]{2,1,0:T(8,128)(2,1)} %param.13) | copy-start | bytes 11010052
  288.5 14.4 %copy-start.3 = (f32[128,4]{0,1:T(4,128)S(1)}, f32[128,4]{0,1:T(4,128)}, u32[]{:S(2)}) copy-start(f32[128,4]{0,1:T(4,128)} %param.12) | copy-start | bytes 6148
  288.5 84.6 %all-to-all-start.1 = ((bf16[128,3,2,1920]{3,2,1,0:T(2,128)(2,1)}), bf16[128,3,2,1920]{3,2,1,0:T(2,128)(2,1)}, u32[]{:S(2)}, u32[]{:S(2)}) async-start(bf16[128,3,2,1920]{3,2,1,0:T(2,128)(2,1)} %reshape.93), calls=%async_computation.2 | async-start | bytes 5898240 | tf_op jit(solution)/shard_map/all_to_all | solution.py:60
Sparse Core Ops, SparseCore 0:
  171.0 23.7 all-gather.2
  257.8 24.9 reduce-scatter.1

commit v3 on v2

v3 whole, which is shorter than its diff:
```python
import jax
import jax.numpy as jnp
from jax import lax
from jax.sharding import PartitionSpec as P


def body(tokens, out_grad, route_ids, route_gates, w_gate, w_up, w_down):
    expert_count = lax.axis_size("expert")
    pair_count = lax.axis_size("hid")
    hid_idx = lax.axis_index("hid")
    tok_rows, model_width = tokens.shape
    top_count = route_ids.shape[1]
    capacity = 3 * tok_rows * top_count // (2 * expert_count)
    slot_count = expert_count * capacity
    half_width = model_width // pair_count
    pair_total = tok_rows * top_count
    flat_ids = route_ids.reshape(-1)
    one_hot = (flat_ids[:, None] == jnp.arange(expert_count, dtype=jnp.int32)[None, :]).astype(
        jnp.int32
    )
    earlier = jnp.cumsum(one_hot, axis=0) - one_hot
    slot_index = jnp.sum(earlier * one_hot, axis=1)
    dest_slot = flat_ids * capacity + slot_index
    slot_pair = jnp.zeros((slot_count,), jnp.int32).at[dest_slot].set(
        jnp.arange(pair_total, dtype=jnp.int32)
    )
    slot_token = slot_pair // top_count
    source = jnp.where(hid_idx == 0, tokens, out_grad)
    quad = (expert_count, capacity // 2, 2)
    send = source[slot_token.reshape(quad)]
    recv = lax.all_to_all(send, "expert", split_axis=0, concat_axis=0, tiled=True)
    both = lax.all_gather(recv, "hid", axis=0, tiled=False)
    rows_x = both[0]
    rows_d = both[1]
    gate_mat = w_gate[0]
    up_mat = w_up[0]
    down_mat = w_down[0]
    gate_pre = jnp.einsum("ejqc,cf->ejqf", rows_x, gate_mat, preferred_element_type=jnp.float32)
    up_pre = jnp.einsum("ejqc,cf->ejqf", rows_x, up_mat, preferred_element_type=jnp.float32)
    grad_hidden = jnp.einsum(
        "ejqc,fc->ejqf", rows_d, down_mat, preferred_element_type=jnp.float32
    )
    sigma_gate = jax.nn.sigmoid(gate_pre)
    act_gate = gate_pre * sigma_gate
    score_part = jnp.sum(act_gate * up_pre * grad_hidden, axis=3)
    grad_gate_pre = (
        grad_hidden * up_pre * sigma_gate * (1.0 + gate_pre * (1.0 - sigma_gate))
    ).astype(jnp.bfloat16)
    grad_up_pre = (grad_hidden * act_gate).astype(jnp.bfloat16)
    grad_part = jnp.einsum(
        "ejqf,cf->ejqc", grad_gate_pre, gate_mat, preferred_element_type=jnp.float32
    ) + jnp.einsum("ejqf,cf->ejqc", grad_up_pre, up_mat, preferred_element_type=jnp.float32)
    grad_share = lax.psum_scatter(grad_part, "hid", scatter_dimension=3, tiled=True).astype(
        jnp.bfloat16
    )
    score_full = lax.psum(score_part, "hid").astype(jnp.bfloat16)
    score_cols = jnp.zeros(quad + (128,), jnp.bfloat16).at[..., 0].set(score_full)
    back_send = jnp.concatenate([grad_share, score_cols], axis=3)
    back = lax.all_to_all(back_send, "expert", split_axis=0, concat_axis=0, tiled=True)
    picked = back[flat_ids, slot_index // 2, slot_index % 2]
    pair_grad = picked[:, :half_width].reshape(tok_rows, top_count, half_width)
    token_grad = jnp.sum(
        pair_grad.astype(jnp.float32) * route_gates[:, :, None], axis=1
    ).astype(jnp.bfloat16)
    gate_grad = picked[:, half_width].reshape(tok_rows, top_count)
    return (token_grad, gate_grad)


def solution(mesh):
    return jax.shard_map(
        body,
        mesh=mesh,
        in_specs=(
            P("expert", None),
            P("expert", None),
            P("expert", None),
            P("expert", None),
            P("expert", None, "hid"),
            P("expert", None, "hid"),
            P("expert", "hid", None),
        ),
        out_specs=(P("expert", "hid"), P("expert", None)),
        check_vma=False,
    )
```

time: 399 us -> 369 us (0.925)
  local copies, waits for them, and re-layouts: 72.8 us -> 45.4 us
  matrix products: 31 us -> 22.3 us
  other arithmetic: 6.83 us -> 12.8 us
    another operation x6 -> x4, local copies, waits for them, and re-layouts: 23.9 us -> 0.22 us  [the longest x1 11.9 us: body(): rows_d = both[1].reshape(slot_count, model_width)]
    reshape x4 -> x2, local copies, waits for them, and re-layouts: 21.5 us -> 0.29 us  [the longest x1 0.19 us: body(): send = source[slot_token.reshape(quad)]]
    gather x2 -> x3, local copies, waits for them, and re-layouts: 8.66 us -> 24.7 us  [the longest x2 16.8 us: body(): send = source[slot_token.reshape(quad)]]
    slice x2 -> x0, local copies, waits for them, and re-layouts: 12.2 us -> none  [the longest x1 10.6 us: body(): rows_x = both[0].reshape(slot_count, model_width)]
    dot_general x6 -> x5, matrix products: 31 us -> 22.3 us  [the longest x1 6.25 us: body(): jnp.einsum('ejqf,cf->ejqc', grad_up_pre, up_mat, preferred_element_type=j...]
    reduce_sum x0 -> x1, other arithmetic: none -> 5.45 us  [body(): jnp.sum(pair_grad.astype(jnp.float32) * route_gates[:, :, None], axis=1)]
    convert_element_type x0 -> x1, local copies, waits for them, and re-layouts: none -> 5.13 us  [body(): pair_grad.astype(jnp.float32) * route_gates[:, :, None]]
    concatenate x0 -> x1, local copies, waits for them, and re-layouts: none -> 4.63 us  [body(): back_send = jnp.concatenate([grad_share, score_cols], axis=3)]
where the time goes in v3:
time: 369 us; the launch traced here: 368 us
  blocking collectives  143 us (39%)
  waiting for transfers between devices  116 us (31%)
  local copies, waits for them, and re-layouts  45.4 us (12%)
  matrix products  22.3 us (6%)
  starting transfers between devices  14.5 us (4%)
  between operations  14.3 us (4%)
  other arithmetic  12.8 us (3%)
    all_to_all x1, blocking collectives, body(): lax.all_to_all(send, 'expert', split_axis=0, concat_axis=0, tiled=True)  140 us
    all_to_all x1, waiting for transfers between devices, body(): lax.all_to_all(back_send, 'expert', split_axis=0, concat_axis=0, tiled=True)  70.4 us
    all_gather x1, waiting for transfers between devices, body(): both = lax.all_gather(recv, 'hid', axis=0, tiled=False)  23.1 us
    reduce_scatter x1, waiting for transfers between devices, body(): lax.psum_scatter(grad_part, 'hid', scatter_dimension=3, tiled=True)  22.5 us
    gather x2, local copies, waits for them, and re-layouts, body(): send = source[slot_token.reshape(quad)]  16.8 us
    all_to_all x1, starting transfers between devices, body(): lax.all_to_all(back_send, 'expert', split_axis=0, concat_axis=0, tiled=True)  14.2 us
    gather x1, local copies, waits for them, and re-layouts, body(): picked = back[flat_ids, slot_index // 2, slot_index % 2]  7.84 us
  transfers between devices with their start and end apart: 3, of which 3 were waited for; matrix products, arithmetic and copies ran while one was open for 0% of the time, Pallas kernels for 0%

profile of v3, /device:TPU:2, one launch (start us, length us, event | category | flops | bytes accessed | tf_op | source)
XLA Modules:
  0.0 368.1 jit_solution(15681189867348111630)
XLA Ops:
  7.2 0.9 copy.22
  9.2 2.4 scatter_custom_fusion
  12.3 5.4 %gather_fusion = bf16[768,3584]{1,0:T(8,128)(2,1)} fusion(bf16[128,3584]{1,0:T(8,128)(2,1)S(1)} %broadcast_select_fusion, s32[1024]{0:T(1024)S(1)} %pad_clamp_fusion), kind=kCustom, calls=%fused_computation | custom fusion | bytes 11013120 | tf_op jit(solution)/shard_map/gather | solution.py:30
  17.7 11.4 %reshape.248 = bf16[128,3,2,3584]{3,2,1,0:T(2,128)(2,1)} reshape(bf16[768,3584]{1,0:T(8,128)(2,1)} %gather_fusion) | data formatting | bytes 11010048 | tf_op jit(solution)/shard_map/gather | solution.py:30
  29.1 140.3 %all_to_all.10 = bf16[128,3,2,3584]{3,2,1,0:T(2,128)(2,1)S(1)} all-to-all(bf16[128,3,2,3584]{3,2,1,0:T(2,128)(2,1)} %reshape.248), channel_id=1, replica_groups=mesh['expert'=128,'hid'=2] {'expert'}, dimensions={0} | all-to-all | bytes 11010048 | tf_op jit(solution)/shard_map/all_to_all | solution.py:31
  169.4 3.0 copy.27
  172.6 23.1 %all-gather.3.cloned.1.call-done = bf16[256,3,2,3584]{3,0,2,1:T(8,128)(2,1)} async-done(((bf16[128,3,2,3584]{3,0,2,1:T(8,128)(2,1)}), bf16[256,3,2,3584]{3,0,2,1:T(8,128)(2,1)}) %all-gather.3.cloned.1.call-update) | async-done | bytes 11010064 | tf_op jit(solution)/shard_map/all_gather | solution.py:32
  195.7 6.2 %fusion.5 = f32[128,3,2,512]{3,0,2,1:T(8,128)S(1)} fusion(bf16[256,3,2,3584]{3,0,2,1:T(8,128)(2,1)} %all-gather.3.cloned.1.call-done, bf16[1,3584,512]{2,1,0:T(8,128)(2,1)} %param.13), kind=kOutput, calls=%fused_computation.10 | convolution fusion | flops 2818572288 | bytes 10747904 | tf_op jit(solution)/shard_map/ejqc,cf->ejqf/dot_general | solution.py:38
  201.9 1.7 copy-done.5
  203.6 3.0 fusion.3
  206.7 3.4 multiply_reduce_fusion.1
  210.0 3.5 fusion.7
  213.5 6.3 %convolution_add_fusion = f32[128,3,2,3584]{3,0,2,1:T(8,128)} fusion(f32[128,3,2,3584]{3,0,2,1:T(8,128)S(1)} %fusion.7, bf16[1,3584,512]{2,1,0:T(8,128)(2,1)S(1)} %copy-done.1, f32[128,3,2,512]{3,0,2,1:T(8,128)S(1)} %get-tuple-element.23, f32[128,3,2,512]{3,0,2,1:T(8,128)S(1)} %fusion.5), kind=kOutput, calls=%fused_computation.3 | convolution fusion | flops 2823684096 | bytes 28835840 | tf_op jit(solution)/shard_map/ejqf,cf->ejqc/dot_general | solution.py:52
  219.8 2.5 psum.7
  222.5 22.5 %reduce-scatter.2.cloned.1.call-done = f32[128,3,2,1792]{3,0,2,1:T(8,128)} async-done(((f32[128,3,2,3584]{3,0,2,1:T(8,128)}), f32[128,3,2,1792]{3,0,2,1:T(8,128)}) %reduce-scatter.2.cloned.1.call-update) | async-done | bytes 5505040 | tf_op jit(solution)/shard_map/reduce_scatter | solution.py:53
  244.9 2.8 convert_element_type.32
  248.1 4.6 %copy.29 = bf16[128,3,2,1920]{3,2,1,0:T(2,128)(2,1)} copy(bf16[128,3,2,1920]{3,0,2,1:T(8,128)(2,1)S(1)} %fusion.13) | data formatting | bytes 5898240 | tf_op jit(solution)/shard_map/concatenate | solution.py:58
  252.7 14.2 %all-to-all-start.1 = ((bf16[128,3,2,1920]{3,2,1,0:T(2,128)(2,1)}), bf16[128,3,2,1920]{3,2,1,0:T(2,128)(2,1)S(1)}, u32[]{:S(2)}, u32[]{:S(2)}) async-start(bf16[128,3,2,1920]{3,2,1,0:T(2,128)(2,1)} %copy.29), calls=%async_computation.2 | async-start | bytes 5898240 | tf_op jit(solution)/shard_map/all_to_all | solution.py:59
  267.1 70.4 %all-to-all-done.1 = bf16[128,3,2,1920]{3,2,1,0:T(2,128)(2,1)S(1)} async-done(((bf16[128,3,2,1920]{3,2,1,0:T(2,128)(2,1)}), bf16[128,3,2,1920]{3,2,1,0:T(2,128)(2,1)S(1)}, u32[]{:S(2)}, u32[]{:S(2)}) %all-to-all-start.1) | async-done | bytes 2949152 | tf_op jit(solution)/shard_map/all_to_all | solution.py:59
  337.5 7.8 %gather_fusion.1 = bf16[512,1920]{1,0:T(8,128)(2,1)} fusion(bf16[128,3,2,1920]{3,2,1,0:T(2,128)(2,1)S(1)} %all-to-all-done.1, s32[512]{0:T(512)S(1)} %bitcast.48), kind=kCustom, calls=%fused_computation.1 | custom fusion | bytes 3938304 | tf_op jit(solution)/shard_map/gather | solution.py:60
  345.3 3.6 slice_convert_fusion
  348.9 1.0 slice_reduce_fusion
  349.9 5.1 %reshape.246 = f32[128,4,1792]{2,1,0:T(4,128)} reshape(f32[512,1792]{1,0:T(8,128)} %slice_convert_fusion) | data formatting | bytes 7340032 | tf_op jit(solution)/shard_map/convert_element_type | solution.py:63
  355.8 5.4 %multiply_reduce_fusion = bf16[128,1792]{1,0:T(8,128)(2,1)} fusion(f32[128,4,1792]{2,1,0:T(4,128)} %reshape.246, f32[128,4]{1,0:T(8,128)S(1)} %copy.30), kind=kLoop, calls=%fused_computation.18 | loop fusion | flops 1605632 | bytes 4130816 | tf_op jit(solution)/shard_map/reduce_sum | solution.py:62
  (42 shorter events, 3.2 us)
Async XLA Ops:
  7.2 5.0 %copy-start.3 = (bf16[128,3584]{1,0:T(8,128)(2,1)S(1)}, bf16[128,3584]{1,0:T(8,128)(2,1)}, u32[]{:S(2)}) copy-start(bf16[128,3584]{1,0:T(8,128)(2,1)} %param.10) | copy-start | bytes 2752516
  7.2 5.0 %copy-start.2 = (bf16[128,3584]{1,0:T(8,128)(2,1)S(1)}, bf16[128,3584]{1,0:T(8,128)(2,1)}, u32[]{:S(2)}) copy-start(bf16[128,3584]{1,0:T(8,128)(2,1)} %param.9) | copy-start | bytes 2752516
  7.2 188.5 %all-gather.3.cloned.1.call-start = ((), (), s32[]{:S(2)}) async-start(), calls=%async_computation.4 | async-start | bytes 16515072 | tf_op jit(solution)/shard_map/all_gather | solution.py:32
  172.4 72.5 %reduce-scatter.2.cloned.1.call-start = ((), (), s32[]{:S(2)}) async-start(), calls=%async_computation.3 | async-start | bytes 16515072 | tf_op jit(solution)/shard_map/reduce_scatter | solution.py:53
  195.7 6.2 %copy-start.1 = (bf16[1,3584,512]{2,1,0:T(8,128)(2,1)S(1)}, bf16[1,3584,512]{2,1,0:T(8,128)(2,1)}, u32[]{:S(2)}) copy-start(bf16[1,3584,512]{2,1,0:T(8,128)(2,1)} %param.14) | copy-start | bytes 11010052
  195.7 7.9 %copy-start.5 = (bf16[256,3,2,3584]{3,0,2,1:T(8,128)(2,1)S(1)}, bf16[256,3,2,3584]{3,0,2,1:T(8,128)(2,1)}, u32[]{:S(2)}) copy-start(bf16[256,3,2,3584]{3,0,2,1:T(8,128)(2,1)} %all-gather.3.cloned.1.call-done) | copy-start | bytes 33030148
  203.6 3.0 copy-start.6
  206.6 3.4 copy-start
  252.7 14.2 %copy-start.4 = (f32[128,4]{0,1:T(4,128)S(1)}, f32[128,4]{0,1:T(4,128)}, u32[]{:S(2)}) copy-start(f32[128,4]{0,1:T(4,128)} %param.12) | copy-start | bytes 6148
  252.7 84.7 %all-to-all-start.1 = ((bf16[128,3,2,1920]{3,2,1,0:T(2,128)(2,1)}), bf16[128,3,2,1920]{3,2,1,0:T(2,128)(2,1)S(1)}, u32[]{:S(2)}, u32[]{:S(2)}) async-start(bf16[128,3,2,1920]{3,2,1,0:T(2,128)(2,1)} %copy.29), calls=%async_computation.2 | async-start | bytes 5898240 | tf_op jit(solution)/shard_map/all_to_all | solution.py:59
Sparse Core Ops, SparseCore 0:
  172.5 23.1 all-gather.2
  219.9 24.9 reduce-scatter.1

commit v4 on v3

--- a/solution.py
+++ b/solution.py
@@ -50,19 +50,22 @@
     grad_part = jnp.einsum(
         "ejqf,cf->ejqc", grad_gate_pre, gate_mat, preferred_element_type=jnp.float32
     ) + jnp.einsum("ejqf,cf->ejqc", grad_up_pre, up_mat, preferred_element_type=jnp.float32)
-    grad_share = lax.psum_scatter(grad_part, "hid", scatter_dimension=3, tiled=True).astype(
-        jnp.bfloat16
+    grad_share = lax.psum_scatter(
+        grad_part.astype(jnp.bfloat16), "hid", scatter_dimension=3, tiled=True
     )
     score_full = lax.psum(score_part, "hid").astype(jnp.bfloat16)
     score_cols = jnp.zeros(quad + (128,), jnp.bfloat16).at[..., 0].set(score_full)
     back_send = jnp.concatenate([grad_share, score_cols], axis=3)
     back = lax.all_to_all(back_send, "expert", split_axis=0, concat_axis=0, tiled=True)
-    picked = back[flat_ids, slot_index // 2, slot_index % 2]
-    pair_grad = picked[:, :half_width].reshape(tok_rows, top_count, half_width)
-    token_grad = jnp.sum(
-        pair_grad.astype(jnp.float32) * route_gates[:, :, None], axis=1
-    ).astype(jnp.bfloat16)
-    gate_grad = picked[:, half_width].reshape(tok_rows, top_count)
+    route_slot = slot_index.reshape(tok_rows, top_count)
+    token_grad = jnp.zeros((tok_rows, half_width), jnp.float32)
+    scores = []
+    for k in range(top_count):
+        row = back[route_ids[:, k], route_slot[:, k] // 2, route_slot[:, k] % 2]
+        token_grad = token_grad + row[:, :half_width].astype(jnp.float32) * route_gates[:, k, None]
+        scores.append(row[:, half_width])
+    token_grad = token_grad.astype(jnp.bfloat16)
+    gate_grad = jnp.stack(scores, axis=1)
     return (token_grad, gate_grad)
 
 

time: 369 us -> 356 us (0.965)
  other arithmetic: 12.8 us -> 6.56 us
  waiting for transfers between devices: 116 us -> 110 us
    reduce_sum x1 -> x0, other arithmetic: 5.45 us -> none  [body(): jnp.sum(pair_grad.astype(jnp.float32) * route_gates[:, :, None], axis=1)]
    convert_element_type x1 -> x0, local copies, waits for them, and re-layouts: 5.13 us -> none  [body(): pair_grad.astype(jnp.float32) * route_gates[:, :, None]]
    reduce_scatter x1, waiting for transfers between devices: 22.5 us -> 17.4 us  [body(): lax.psum_scatter(grad_part.astype(jnp.bfloat16), 'hid', scatter_dimension...]
    convert_element_type x2 -> x1, other arithmetic: 6.38 us -> 2.49 us  [body(): token_grad = token_grad.astype(jnp.bfloat16)]
    gather x1 -> x4, local copies, waits for them, and re-layouts: 7.84 us -> 9.81 us  [body(): row = back[route_ids[:, k], route_slot[:, k] // 2, route_slot[:, k] % 2]]
where the time goes in v4:
time: 356 us; the launch traced here: 355 us
  blocking collectives  143 us (40%)
  waiting for transfers between devices  110 us (31%)
  local copies, waits for them, and re-layouts  43.6 us (12%)
  matrix products  23 us (6%)
  starting transfers between devices  14.3 us (4%)
  between operations  14.3 us (4%)
  other arithmetic  6.56 us (2%)
    all_to_all x1, blocking collectives, body(): lax.all_to_all(send, 'expert', split_axis=0, concat_axis=0, tiled=True)  140 us
    all_to_all x1, waiting for transfers between devices, body(): lax.all_to_all(back_send, 'expert', split_axis=0, concat_axis=0, tiled=True)  69.9 us
    all_gather x1, waiting for transfers between devices, body(): both = lax.all_gather(recv, 'hid', axis=0, tiled=False)  23.1 us
    reduce_scatter x1, waiting for transfers between devices, body(): lax.psum_scatter(grad_part.astype(jnp.bfloat16), 'hid', scatter_dimension...  17.4 us
    gather x2, local copies, waits for them, and re-layouts, body(): send = source[slot_token.reshape(quad)]  16.9 us
    all_to_all x1, starting transfers between devices, body(): lax.all_to_all(back_send, 'expert', split_axis=0, concat_axis=0, tiled=True)  14 us
    gather x4, local copies, waits for them, and re-layouts, body(): row = back[route_ids[:, k], route_slot[:, k] // 2, route_slot[:, k] % 2]  9.81 us
  transfers between devices with their start and end apart: 3, of which 3 were waited for; matrix products, arithmetic and copies ran while one was open for 0% of the time, Pallas kernels for 0%

profile of v4, /device:TPU:2, one launch (start us, length us, event | category | flops | bytes accessed | tf_op | source)
XLA Modules:
  0.0 354.9 jit_solution(4023039571031431696)
XLA Ops:
  7.2 0.9 copy.111
  10.0 2.4 scatter_custom_fusion
  13.0 5.4 %gather_fusion = bf16[768,3584]{1,0:T(8,128)(2,1)} fusion(bf16[128,3584]{1,0:T(8,128)(2,1)S(1)} %broadcast_select_fusion, s32[1024]{0:T(1024)S(1)} %pad_clamp_fusion), kind=kCustom, calls=%fused_computation | custom fusion | bytes 11013120 | tf_op jit(solution)/shard_map/gather | solution.py:30
  18.5 11.4 %reshape.128 = bf16[128,3,2,3584]{3,2,1,0:T(2,128)(2,1)} reshape(bf16[768,3584]{1,0:T(8,128)(2,1)} %gather_fusion) | data formatting | bytes 11010048 | tf_op jit(solution)/shard_map/gather | solution.py:30
  29.9 140.3 %all_to_all.10 = bf16[128,3,2,3584]{3,2,1,0:T(2,128)(2,1)S(1)} all-to-all(bf16[128,3,2,3584]{3,2,1,0:T(2,128)(2,1)} %reshape.128), channel_id=1, replica_groups=mesh['expert'=128,'hid'=2] {'expert'}, dimensions={0} | all-to-all | bytes 11010048 | tf_op jit(solution)/shard_map/all_to_all | solution.py:31
  170.2 3.0 copy.115
  173.4 23.1 %all-gather.3.cloned.1.call-done = bf16[256,3,2,3584]{3,0,2,1:T(8,128)(2,1)} async-done(((bf16[128,3,2,3584]{3,0,2,1:T(8,128)(2,1)}), bf16[256,3,2,3584]{3,0,2,1:T(8,128)(2,1)}) %all-gather.3.cloned.1.call-update) | async-done | bytes 11010064 | tf_op jit(solution)/shard_map/all_gather | solution.py:32
  196.5 6.2 %fusion.5 = f32[128,3,2,512]{3,0,2,1:T(8,128)S(1)} fusion(bf16[256,3,2,3584]{3,0,2,1:T(8,128)(2,1)} %all-gather.3.cloned.1.call-done, bf16[1,3584,512]{2,1,0:T(8,128)(2,1)} %param.13), kind=kOutput, calls=%fused_computation.13 | convolution fusion | flops 2818572288 | bytes 10747904 | tf_op jit(solution)/shard_map/ejqc,cf->ejqf/dot_general | solution.py:38
  202.7 1.7 copy-done.6
  204.4 3.0 fusion.3
  207.4 3.3 multiply_reduce_fusion
  210.8 3.5 fusion.7
  214.3 7.0 %add_convert_fusion = bf16[128,3,2,3584]{3,0,2,1:T(8,128)(2,1)} fusion(f32[128,3,2,3584]{3,0,2,1:T(8,128)S(1)} %fusion.7, bf16[1,3584,512]{2,1,0:T(8,128)(2,1)} %param.14, f32[128,3,2,512]{3,0,2,1:T(8,128)S(1)} %get-tuple-element.33, f32[128,3,2,512]{3,0,2,1:T(8,128)S(1)} %fusion.5), kind=kOutput, calls=%fused_computation.6 | convolution fusion | flops 2826436608 | bytes 23330816 | tf_op jit(solution)/shard_map/ejqf,cf->ejqc/dot_general | solution.py:52
  221.3 2.5 psum.7
  224.0 17.4 %reduce-scatter.2.cloned.1.call-done = bf16[128,3,2,1792]{3,0,2,1:T(8,128)(2,1)} async-done(((bf16[128,3,2,3584]{3,0,2,1:T(8,128)(2,1)}), bf16[128,3,2,1792]{3,0,2,1:T(8,128)(2,1)}) %reduce-scatter.2.cloned.1.call-update) | async-done | bytes 2752528 | tf_op jit(solution)/shard_map/reduce_scatter | solution.py:53
  241.3 2.1 fusion.13
  243.4 4.6 %copy.117 = bf16[128,3,2,1920]{3,2,1,0:T(2,128)(2,1)} copy(bf16[128,3,2,1920]{3,0,2,1:T(8,128)(2,1)S(1)} %fusion.13) | data formatting | bytes 5898240 | tf_op jit(solution)/shard_map/concatenate | solution.py:58
  248.0 14.0 %all-to-all-start.1 = ((bf16[128,3,2,1920]{3,2,1,0:T(2,128)(2,1)}), bf16[128,3,2,1920]{3,2,1,0:T(2,128)(2,1)S(1)}, u32[]{:S(2)}, u32[]{:S(2)}) async-start(bf16[128,3,2,1920]{3,2,1,0:T(2,128)(2,1)} %copy.117), calls=%async_computation.2 | async-start | bytes 5898240 | tf_op jit(solution)/shard_map/all_to_all | solution.py:59
  262.6 69.9 %all-to-all-done.1 = bf16[128,3,2,1920]{3,2,1,0:T(2,128)(2,1)S(1)} async-done(((bf16[128,3,2,1920]{3,2,1,0:T(2,128)(2,1)}), bf16[128,3,2,1920]{3,2,1,0:T(2,128)(2,1)S(1)}, u32[]{:S(2)}, u32[]{:S(2)}) %all-to-all-start.1) | async-done | bytes 2949152 | tf_op jit(solution)/shard_map/all_to_all | solution.py:59
  332.5 1.9 gather_fusion.1
  334.5 2.7 gather_fusion.2
  338.0 2.7 gather_fusion.3
  341.5 2.6 gather_fusion.4
  345.5 2.5 add_convert_fusion.1
  (59 shorter events, 6.6 us)
Async XLA Ops:
  7.2 5.7 %copy-start.3 = (bf16[128,3584]{1,0:T(8,128)(2,1)S(1)}, bf16[128,3584]{1,0:T(8,128)(2,1)}, u32[]{:S(2)}) copy-start(bf16[128,3584]{1,0:T(8,128)(2,1)} %param.10) | copy-start | bytes 2752516
  7.2 5.7 %copy-start.2 = (bf16[128,3584]{1,0:T(8,128)(2,1)S(1)}, bf16[128,3584]{1,0:T(8,128)(2,1)}, u32[]{:S(2)}) copy-start(bf16[128,3584]{1,0:T(8,128)(2,1)} %param.9) | copy-start | bytes 2752516
  7.2 189.3 %all-gather.3.cloned.1.call-start = ((), (), s32[]{:S(2)}) async-start(), calls=%async_computation.4 | async-start | bytes 16515072 | tf_op jit(solution)/shard_map/all_gather | solution.py:32
  173.2 68.1 %reduce-scatter.2.cloned.1.call-start = ((), (), s32[]{:S(2)}) async-start(), calls=%async_computation.3 | async-start | bytes 8257536 | tf_op jit(solution)/shard_map/reduce_scatter | solution.py:53
  196.5 6.2 %copy-start.1 = (bf16[1,3584,512]{2,1,0:T(8,128)(2,1)S(1)}, bf16[1,3584,512]{2,1,0:T(8,128)(2,1)}, u32[]{:S(2)}) copy-start(bf16[1,3584,512]{2,1,0:T(8,128)(2,1)} %param.14) | copy-start | bytes 11010052
  196.5 7.9 %copy-start.6 = (bf16[256,3,2,3584]{3,0,2,1:T(8,128)(2,1)S(1)}, bf16[256,3,2,3584]{3,0,2,1:T(8,128)(2,1)}, u32[]{:S(2)}) copy-start(bf16[256,3,2,3584]{3,0,2,1:T(8,128)(2,1)} %all-gather.3.cloned.1.call-done) | copy-start | bytes 33030148
  204.4 3.0 copy-start.7
  207.4 3.4 copy-start
  248.0 14.6 %copy-start.5 = (f32[128,4]{0,1:T(4,128)S(1)}, f32[128,4]{0,1:T(4,128)}, u32[]{:S(2)}) copy-start(f32[128,4]{0,1:T(4,128)} %param.12) | copy-start | bytes 6148
  248.0 14.6 %copy-start.4 = (s32[128,4]{0,1:T(4,128)S(1)}, s32[128,4]{0,1:T(4,128)}, u32[]{:S(2)}) copy-start(s32[128,4]{0,1:T(4,128)} %param.11) | copy-start | bytes 6148
  248.0 84.5 %all-to-all-start.1 = ((bf16[128,3,2,1920]{3,2,1,0:T(2,128)(2,1)}), bf16[128,3,2,1920]{3,2,1,0:T(2,128)(2,1)S(1)}, u32[]{:S(2)}, u32[]{:S(2)}) async-start(bf16[128,3,2,1920]{3,2,1,0:T(2,128)(2,1)} %copy.117), calls=%async_computation.2 | async-start | bytes 5898240 | tf_op jit(solution)/shard_map/all_to_all | solution.py:59
Sparse Core Ops, SparseCore 0:
  173.3 23.1 all-gather.2
  221.4 19.8 reduce-scatter.1

commit v5 on v4

--- a/solution.py
+++ b/solution.py
@@ -29,9 +29,11 @@
     quad = (expert_count, capacity // 2, 2)
     send = source[slot_token.reshape(quad)]
     recv = lax.all_to_all(send, "expert", split_axis=0, concat_axis=0, tiled=True)
-    both = lax.all_gather(recv, "hid", axis=0, tiled=False)
-    rows_x = both[0]
-    rows_d = both[1]
+    swap = [(0, 1), (1, 0)]
+    other = lax.ppermute(recv, "hid", swap)
+    first = hid_idx == 0
+    rows_x = jnp.where(first, recv, other)
+    rows_d = jnp.where(first, other, recv)
     gate_mat = w_gate[0]
     up_mat = w_up[0]
     down_mat = w_down[0]
@@ -50,9 +52,14 @@
     grad_part = jnp.einsum(
         "ejqf,cf->ejqc", grad_gate_pre, gate_mat, preferred_element_type=jnp.float32
     ) + jnp.einsum("ejqf,cf->ejqc", grad_up_pre, up_mat, preferred_element_type=jnp.float32)
-    grad_share = lax.psum_scatter(
-        grad_part.astype(jnp.bfloat16), "hid", scatter_dimension=3, tiled=True
-    )
+    own_half = lax.dynamic_slice_in_dim(grad_part, hid_idx * half_width, half_width, axis=3)
+    give_half = lax.dynamic_slice_in_dim(
+        grad_part, (1 - hid_idx) * half_width, half_width, axis=3
+    ).astype(jnp.bfloat16)
+    got_half = lax.ppermute(give_half, "hid", swap)
+    grad_share = (
+        own_half.astype(jnp.bfloat16).astype(jnp.float32) + got_half.astype(jnp.float32)
+    ).astype(jnp.bfloat16)
     score_full = lax.psum(score_part, "hid").astype(jnp.bfloat16)
     score_cols = jnp.zeros(quad + (128,), jnp.bfloat16).at[..., 0].set(score_full)
     back_send = jnp.concatenate([grad_share, score_cols], axis=3)

time: 356 us -> 315 us (0.88)
  waiting for transfers between devices: 110 us -> 79.3 us
  between operations: 14.3 us -> 0.91 us
  other arithmetic: 6.56 us -> 18.2 us
  starting transfers between devices: 14.3 us -> 8.12 us
    all_gather x1 -> x0, waiting for transfers between devices: 23.1 us -> none  [body(): both = lax.all_gather(recv, 'hid', axis=0, tiled=False)]
    reduce_scatter x1 -> x0, waiting for transfers between devices: 17.4 us -> none  [body(): lax.psum_scatter(grad_part.astype(jnp.bfloat16), 'hid', scatter_dimension...]
    select_n x0 -> x1, other arithmetic: none -> 11 us  [body(): rows_x = jnp.where(first, recv, other)]
    ppermute x0 -> x2, waiting for transfers between devices: none -> 9.37 us  [the longest x1 9.37 us: body(): other = lax.ppermute(recv, 'hid', swap)]
    all_to_all x1, starting transfers between devices: 14 us -> 7.98 us  [body(): lax.all_to_all(back_send, 'expert', split_axis=0, concat_axis=0, tiled=True)]
  transfers between devices with their start and end apart: 3 -> 3, of which waited for: 3 -> 2; matrix products, arithmetic and copies ran while one was open for 0% -> 0% of each run, Pallas kernels for 0% -> 0%
where the time goes in v5:
time: 315 us; the launch traced here: 314 us
  blocking collectives  146 us (46%)
  waiting for transfers between devices  79.3 us (25%)
  local copies, waits for them, and re-layouts  42.4 us (13%)
  matrix products  19.8 us (6%)
  other arithmetic  18.2 us (6%)
  starting transfers between devices  8.12 us (3%)
    all_to_all x1, blocking collectives, body(): lax.all_to_all(send, 'expert', split_axis=0, concat_axis=0, tiled=True)  140 us
    all_to_all x1, waiting for transfers between devices, body(): lax.all_to_all(back_send, 'expert', split_axis=0, concat_axis=0, tiled=True)  69.9 us
    gather x2, local copies, waits for them, and re-layouts, body(): send = source[slot_token.reshape(quad)]  16.9 us
    select_n x1, other arithmetic, body(): rows_x = jnp.where(first, recv, other)  11 us
    gather x4, local copies, waits for them, and re-layouts, body(): row = back[route_ids[:, k], route_slot[:, k] // 2, route_slot[:, k] % 2]  9.8 us
    ppermute x1, waiting for transfers between devices, body(): other = lax.ppermute(recv, 'hid', swap)  9.37 us
    all_to_all x1, starting transfers between devices, body(): lax.all_to_all(back_send, 'expert', split_axis=0, concat_axis=0, tiled=True)  7.98 us
    dot_general x1, matrix products, body(): jnp.einsum('ejqf,cf->ejqc', grad_up_pre, up_mat, preferred_element_type=j...  6.94 us
  transfers between devices with their start and end apart: 3, of which 2 were waited for; matrix products, arithmetic and copies ran while one was open for 0% of the time, Pallas kernels for 0%

profile of v5, /device:TPU:2, one launch (start us, length us, event | category | flops | bytes accessed | tf_op | source)
XLA Modules:
  0.0 314.4 jit_solution(17516337414373708614)
XLA Ops:
  0.6 0.9 copy.114
  3.4 2.4 scatter_custom_fusion
  6.4 5.5 %gather_fusion = bf16[768,3584]{1,0:T(8,128)(2,1)} fusion(bf16[128,3584]{1,0:T(8,128)(2,1)S(1)} %broadcast_select_fusion.2, s32[1024]{0:T(1024)S(1)} %pad_clamp_fusion), kind=kCustom, calls=%fused_computation | custom fusion | bytes 11013120 | tf_op jit(solution)/shard_map/gather | solution.py:30
  11.9 11.4 %reshape.128 = bf16[128,3,2,3584]{3,2,1,0:T(2,128)(2,1)} reshape(bf16[768,3584]{1,0:T(8,128)(2,1)} %gather_fusion) | data formatting | bytes 11010048 | tf_op jit(solution)/shard_map/gather | solution.py:30
  23.3 140.4 %all_to_all.10 = bf16[128,3,2,3584]{3,2,1,0:T(2,128)(2,1)} all-to-all(bf16[128,3,2,3584]{3,2,1,0:T(2,128)(2,1)} %reshape.128), channel_id=1, replica_groups=mesh['expert'=128,'hid'=2] {'expert'}, dimensions={0} | all-to-all | bytes 11010048 | tf_op jit(solution)/shard_map/all_to_all | solution.py:31
  163.7 9.4 %collective-permute-done = bf16[128,3,2,3584]{3,2,1,0:T(2,128)(2,1)} collective-permute-done((bf16[128,3,2,3584]{3,2,1,0:T(2,128)(2,1)}, bf16[128,3,2,3584]{3,2,1,0:T(2,128)(2,1)}, u32[]{:S(2)}, u32[]{:S(2)}) %collective-permute-start) | collective-permute-done | bytes 5505056 | tf_op jit(solution)/shard_map/ppermute | solution.py:33
  173.1 11.0 %broadcast_select_fusion = (bf16[128,3,2,3584]{3,2,1,0:T(2,128)(2,1)S(1)}, bf16[128,3,2,3584]{3,2,1,0:T(2,128)(2,1)S(1)}) fusion(bf16[128,3,2,3584]{3,2,1,0:T(2,128)(2,1)} %all_to_all.10, bf16[128,3,2,3584]{3,2,1,0:T(2,128)(2,1)} %collective-permute-done, pred[]{:T(512)S(6)} %eq.34), kind=kLoop, calls=%fused_computation.6 | loop fusion | flops 5505024 | bytes 22020096 | tf_op jit(solution)/shard_map/jit(_where)/select_n | solution.py:35
  184.2 3.0 fusion.3
  187.2 3.0 fusion.5
  190.2 3.4 %multiply_reduce_fusion = (f32[128,3,2]{0,2,1:T(2,128)S(1)}, f32[128,3,2,512]{3,0,2,1:T(8,128)S(1)}) fusion(f32[128,3,2,512]{3,0,2,1:T(8,128)S(1)} %fusion.5, f32[128,3,2,512]{3,0,2,1:T(8,128)S(1)} %fusion.3, bf16[1,512,3584]{2,1,0:T(8,128)(2,1)S(1)} %copy-done.6, bf16[128,3,2,3584]{3,2,1,0:T(2,128)(2,1)S(1)} %get-tuple-element.21), kind=kOutput, calls=%fused_computation.27 | convolution fusion | flops 2821324032 | bytes 13896704 | tf_op jit(solution)/shard_map/ejqc,fc->ejqf/dot_general | solution.py:42
  193.6 3.5 %fusion.7 = f32[128,3,2,3584]{3,0,2,1:T(8,128)S(1)} fusion(bf16[1,3584,512]{2,1,0:T(8,128)(2,1)S(1)} %copy-done, f32[128,3,2,512]{3,0,2,1:T(8,128)S(1)} %fusion.3, f32[128,3,2,512]{3,0,2,1:T(8,128)S(1)} %get-tuple-element.35, f32[128,3,2,512]{3,0,2,1:T(8,128)S(1)} %fusion.5), kind=kOutput, calls=%fused_computation.20 | convolution fusion | flops 2822504448 | bytes 19398656 | tf_op jit(solution)/shard_map/ejqf,cf->ejqc/dot_general | solution.py:52
  197.1 6.9 %convolution_add_fusion = bf16[128,3,2,3584]{3,0,2,1:T(8,128)(2,1)} fusion(f32[128,3,2,3584]{3,0,2,1:T(8,128)S(1)} %fusion.7, bf16[1,3584,512]{2,1,0:T(8,128)(2,1)} %param.14, f32[128,3,2,512]{3,0,2,1:T(8,128)S(1)} %get-tuple-element.35, f32[128,3,2,512]{3,0,2,1:T(8,128)S(1)} %fusion.3), kind=kOutput, calls=%fused_computation.8 | convolution fusion | flops 2826436608 | bytes 23330816 | tf_op jit(solution)/shard_map/ejqf,cf->ejqc/dot_general | solution.py:54
  204.0 3.5 %dynamic-slice_convert_fusion = bf16[128,3,2,1792]{3,0,2,1:T(8,128)(2,1)} fusion(bf16[128,3,2,3584]{3,0,2,1:T(8,128)(2,1)} %convolution_add_fusion, s32[]{:T(128)S(6)} %select_n.149), kind=kLoop, calls=%fused_computation.14 | loop fusion | bytes 5505028 | tf_op jit(solution)/shard_map/convert_element_type | solution.py:58
  207.7 5.2 %psum.7 = bf16[128,3,2]{0,2,1:T(2,128)(2,1)S(1)} all-reduce(f32[128,3,2]{0,2,1:T(2,128)S(1)} %get-tuple-element.34), channel_id=1, replica_groups=mesh['expert'=128,'hid'=2] {'hid'}, use_global_device_ids=true, to_apply=%region_5.6 | all-reduce | flops 768 | bytes 4608 | tf_op jit(solution)/shard_map/psum | solution.py:63
  213.0 2.4 add_convert_fusion
  215.8 4.6 %copy.122 = bf16[128,3,2,1920]{3,2,1,0:T(2,128)(2,1)} copy(bf16[128,3,2,1920]{3,0,2,1:T(8,128)(2,1)S(1)} %fusion.13) | data formatting | bytes 5898240 | tf_op jit(solution)/shard_map/concatenate | solution.py:65
  220.4 8.0 %all-to-all-start.1 = ((bf16[128,3,2,1920]{3,2,1,0:T(2,128)(2,1)}), bf16[128,3,2,1920]{3,2,1,0:T(2,128)(2,1)S(1)}, u32[]{:S(2)}, u32[]{:S(2)}) async-start(bf16[128,3,2,1920]{3,2,1,0:T(2,128)(2,1)} %copy.122), calls=%async_computation.1 | async-start | bytes 5898240 | tf_op jit(solution)/shard_map/all_to_all | solution.py:66
  229.0 69.9 %all-to-all-done.1 = bf16[128,3,2,1920]{3,2,1,0:T(2,128)(2,1)S(1)} async-done(((bf16[128,3,2,1920]{3,2,1,0:T(2,128)(2,1)}), bf16[128,3,2,1920]{3,2,1,0:T(2,128)(2,1)S(1)}, u32[]{:S(2)}, u32[]{:S(2)}) %all-to-all-start.1) | async-done | bytes 2949152 | tf_op jit(solution)/shard_map/all_to_all | solution.py:66
  298.9 1.9 gather_fusion.1
  300.9 2.7 gather_fusion.2
  303.5 0.8 slice.140
  304.3 2.7 gather_fusion.3
  307.8 2.6 gather_fusion.4
  311.9 2.5 add_convert_fusion.1
  (57 shorter events, 6.0 us)
Async XLA Ops:
  0.6 5.7 %copy-start.3 = (bf16[128,3584]{1,0:T(8,128)(2,1)S(1)}, bf16[128,3584]{1,0:T(8,128)(2,1)}, u32[]{:S(2)}) copy-start(bf16[128,3584]{1,0:T(8,128)(2,1)} %param.10) | copy-start | bytes 2752516
  0.6 5.7 %copy-start.2 = (bf16[128,3584]{1,0:T(8,128)(2,1)S(1)}, bf16[128,3584]{1,0:T(8,128)(2,1)}, u32[]{:S(2)}) copy-start(bf16[128,3584]{1,0:T(8,128)(2,1)} %param.9) | copy-start | bytes 2752516
  163.7 9.4 %collective-permute-start = (bf16[128,3,2,3584]{3,2,1,0:T(2,128)(2,1)}, bf16[128,3,2,3584]{3,2,1,0:T(2,128)(2,1)}, u32[]{:S(2)}, u32[]{:S(2)}) collective-permute-start(bf16[128,3,2,3584]{3,2,1,0:T(2,128)(2,1)} %all_to_all.10), channel_id=1, source_target_pairs={{0,1},{1,0},{2,3},{3,2},{4,5},{5,4},{6,7},{7,6},{8,9},{9,8},{10,11... | collective-permute-start | bytes 16515080 | tf_op jit(solution)/shard_map/ppermute | solution.py:33
  163.7 20.4 %copy-start = (bf16[1,3584,512]{2,1,0:T(8,128)(2,1)S(1)}, bf16[1,3584,512]{2,1,0:T(8,128)(2,1)}, u32[]{:S(2)}) copy-start(bf16[1,3584,512]{2,1,0:T(8,128)(2,1)} %param.13) | copy-start | bytes 11010052
  184.2 3.0 copy-start.1
  187.2 3.0 copy-start.6
  207.5 5.5 %collective-permute-start.1 = (bf16[128,3,2,1792]{3,0,2,1:T(8,128)(2,1)}, bf16[128,3,2,1792]{3,0,2,1:T(8,128)(2,1)S(1)}, u32[]{:S(2)}, u32[]{:S(2)}) collective-permute-start(bf16[128,3,2,1792]{3,0,2,1:T(8,128)(2,1)} %dynamic-slice_convert_fusion), channel_id=1, source_target_pairs={{0,1},{1,0},{2,3},{3,2},{4,5},{5,4},{6,7},{7,6},{8,9},{9,8},{10,11... | collective-permute-start | bytes 8257544 | tf_op jit(solution)/shard_map/ppermute | solution.py:59
  220.4 8.5 %copy-start.5 = (f32[128,4]{0,1:T(4,128)S(1)}, f32[128,4]{0,1:T(4,128)}, u32[]{:S(2)}) copy-start(f32[128,4]{0,1:T(4,128)} %param.12) | copy-start | bytes 6148
  220.4 8.6 %copy-start.4 = (s32[128,4]{0,1:T(4,128)S(1)}, s32[128,4]{0,1:T(4,128)}, u32[]{:S(2)}) copy-start(s32[128,4]{0,1:T(4,128)} %param.11) | copy-start | bytes 6148
  220.4 78.5 %all-to-all-start.1 = ((bf16[128,3,2,1920]{3,2,1,0:T(2,128)(2,1)}), bf16[128,3,2,1920]{3,2,1,0:T(2,128)(2,1)S(1)}, u32[]{:S(2)}, u32[]{:S(2)}) async-start(bf16[128,3,2,1920]{3,2,1,0:T(2,128)(2,1)} %copy.122), calls=%async_computation.1 | async-start | bytes 5898240 | tf_op jit(solution)/shard_map/all_to_all | solution.py:66

commit v6 on v5

--- a/solution.py
+++ b/solution.py
@@ -32,26 +32,35 @@
     swap = [(0, 1), (1, 0)]
     other = lax.ppermute(recv, "hid", swap)
     first = hid_idx == 0
-    rows_x = jnp.where(first, recv, other)
-    rows_d = jnp.where(first, other, recv)
     gate_mat = w_gate[0]
     up_mat = w_up[0]
     down_mat = w_down[0]
-    gate_pre = jnp.einsum("ejqc,cf->ejqf", rows_x, gate_mat, preferred_element_type=jnp.float32)
-    up_pre = jnp.einsum("ejqc,cf->ejqf", rows_x, up_mat, preferred_element_type=jnp.float32)
-    grad_hidden = jnp.einsum(
-        "ejqc,fc->ejqf", rows_d, down_mat, preferred_element_type=jnp.float32
+
+    def expert_math(rows_x, rows_d):
+        gate_pre = jnp.einsum(
+            "ejqc,cf->ejqf", rows_x, gate_mat, preferred_element_type=jnp.float32
+        )
+        up_pre = jnp.einsum("ejqc,cf->ejqf", rows_x, up_mat, preferred_element_type=jnp.float32)
+        grad_hidden = jnp.einsum(
+            "ejqc,fc->ejqf", rows_d, down_mat, preferred_element_type=jnp.float32
+        )
+        sigma_gate = jax.nn.sigmoid(gate_pre)
+        act_gate = gate_pre * sigma_gate
+        score_part = jnp.sum(act_gate * up_pre * grad_hidden, axis=3)
+        grad_gate_pre = (
+            grad_hidden * up_pre * sigma_gate * (1.0 + gate_pre * (1.0 - sigma_gate))
+        ).astype(jnp.bfloat16)
+        grad_up_pre = (grad_hidden * act_gate).astype(jnp.bfloat16)
+        grad_part = jnp.einsum(
+            "ejqf,cf->ejqc", grad_gate_pre, gate_mat, preferred_element_type=jnp.float32
+        ) + jnp.einsum(
+            "ejqf,cf->ejqc", grad_up_pre, up_mat, preferred_element_type=jnp.float32
+        )
+        return score_part, grad_part
+
+    score_part, grad_part = lax.cond(
+        first, expert_math, lambda a, b: expert_math(b, a), recv, other
     )
-    sigma_gate = jax.nn.sigmoid(gate_pre)
-    act_gate = gate_pre * sigma_gate
-    score_part = jnp.sum(act_gate * up_pre * grad_hidden, axis=3)
-    grad_gate_pre = (
-        grad_hidden * up_pre * sigma_gate * (1.0 + gate_pre * (1.0 - sigma_gate))
-    ).astype(jnp.bfloat16)
-    grad_up_pre = (grad_hidden * act_gate).astype(jnp.bfloat16)
-    grad_part = jnp.einsum(
-        "ejqf,cf->ejqc", grad_gate_pre, gate_mat, preferred_element_type=jnp.float32
-    ) + jnp.einsum("ejqf,cf->ejqc", grad_up_pre, up_mat, preferred_element_type=jnp.float32)
     own_half = lax.dynamic_slice_in_dim(grad_part, hid_idx * half_width, half_width, axis=3)
     give_half = lax.dynamic_slice_in_dim(
         grad_part, (1 - hid_idx) * half_width, half_width, axis=3
@@ -60,7 +69,7 @@
     grad_share = (
         own_half.astype(jnp.bfloat16).astype(jnp.float32) + got_half.astype(jnp.float32)
     ).astype(jnp.bfloat16)
-    score_full = lax.psum(score_part, "hid").astype(jnp.bfloat16)
+    score_full = (score_part + lax.ppermute(score_part, "hid", swap)).astype(jnp.bfloat16)
     score_cols = jnp.zeros(quad + (128,), jnp.bfloat16).at[..., 0].set(score_full)
     back_send = jnp.concatenate([grad_share, score_cols], axis=3)
     back = lax.all_to_all(back_send, "expert", split_axis=0, concat_axis=0, tiled=True)

time: 315 us -> 333 us (1.057); the launches traced: 314 us -> 327 us
  matrix products: 19.8 us -> 30.7 us
  loops' own time: 0 us -> 8.82 us
  other arithmetic: 18.2 us -> 11.5 us
  blocking collectives: 146 us -> 140 us
    select_n x1 -> x0, other arithmetic: 11 us -> none  [body(): rows_x = jnp.where(first, recv, other)]
    dot_general x5, matrix products: 19.8 us -> 30.7 us  [the longest x1 8.19 us: expert_math(): jnp.einsum('ejqc,cf->ejqf', rows_x, gate_mat, preferred_element_type=jnp....]
    another operation x0 -> x1, loops' own time: none -> 8.82 us  [body(): lax.cond(first, expert_math, lambda a, b: expert_math(b, a), recv, other)]
    psum x1 -> x0, blocking collectives: 5.2 us -> none  [body(): score_full = lax.psum(score_part, 'hid').astype(jnp.bfloat16)]
  transfers between devices with their start and end apart: 3 -> 4, of which waited for: 2 -> 3; matrix products, arithmetic and copies ran while one was open for 0% -> 1% of each run, Pallas kernels for 0% -> 0%
where the time goes in v6:
time: 333 us; the launch traced here: 327 us
  blocking collectives  140 us (42%)
  waiting for transfers between devices  81.6 us (25%)
  local copies, waits for them, and re-layouts  43.1 us (13%)
  matrix products  30.7 us (9%)
  other arithmetic  11.5 us (3%)
  starting transfers between devices  9.23 us (3%)
  loops' own time  8.82 us (3%)
    all_to_all x1, blocking collectives, body(): lax.all_to_all(send, 'expert', split_axis=0, concat_axis=0, tiled=True)  140 us
    all_to_all x1, waiting for transfers between devices, body(): lax.all_to_all(back_send, 'expert', split_axis=0, concat_axis=0, tiled=True)  69.8 us
    gather x2, local copies, waits for them, and re-layouts, body(): send = source[slot_token.reshape(quad)]  16.8 us
    gather x4, local copies, waits for them, and re-layouts, body(): row = back[route_ids[:, k], route_slot[:, k] // 2, route_slot[:, k] % 2]  9.8 us
    ppermute x1, waiting for transfers between devices, body(): other = lax.ppermute(recv, 'hid', swap)  9.37 us
    another operation x1, loops' own time, body(): lax.cond(first, expert_math, lambda a, b: expert_math(b, a), recv, other)  8.82 us
    all_to_all x1, starting transfers between devices, body(): lax.all_to_all(back_send, 'expert', split_axis=0, concat_axis=0, tiled=True)  8.38 us
    dot_general x1, matrix products, expert_math(): jnp.einsum('ejqc,cf->ejqf', rows_x, gate_mat, preferred_element_type=jnp....  8.19 us
  transfers between devices with their start and end apart: 4, of which 3 were waited for; matrix products, arithmetic and copies ran while one was open for 1% of the time, Pallas kernels for 0%

profile of v6, /device:TPU:2, one launch (start us, length us, event | category | flops | bytes accessed | tf_op | source)
XLA Modules:
  0.0 326.7 jit_solution(14564404553087902406)
XLA Ops:
  3.4 2.4 scatter_custom_fusion
  6.4 5.4 %gather_fusion = bf16[768,3584]{1,0:T(8,128)(2,1)} fusion(bf16[128,3584]{1,0:T(8,128)(2,1)S(1)} %broadcast_select_fusion, s32[1024]{0:T(1024)S(1)} %pad_clamp_fusion), kind=kCustom, calls=%fused_computation | custom fusion | bytes 11013120 | tf_op jit(solution)/shard_map/gather | solution.py:30
  11.9 11.4 %reshape.128 = bf16[128,3,2,3584]{3,2,1,0:T(2,128)(2,1)} reshape(bf16[768,3584]{1,0:T(8,128)(2,1)} %gather_fusion) | data formatting | bytes 11010048 | tf_op jit(solution)/shard_map/gather | solution.py:30
  23.3 140.4 %all_to_all.10 = bf16[128,3,2,3584]{3,2,1,0:T(2,128)(2,1)} all-to-all(bf16[128,3,2,3584]{3,2,1,0:T(2,128)(2,1)} %reshape.128), channel_id=1, replica_groups=mesh['expert'=128,'hid'=2] {'expert'}, dimensions={0} | all-to-all | bytes 11010048 | tf_op jit(solution)/shard_map/all_to_all | solution.py:31
  163.7 9.4 %collective-permute-done = bf16[128,3,2,3584]{3,2,1,0:T(2,128)(2,1)} collective-permute-done((bf16[128,3,2,3584]{3,2,1,0:T(2,128)(2,1)}, bf16[128,3,2,3584]{3,2,1,0:T(2,128)(2,1)}, u32[]{:S(2)}, u32[]{:S(2)}) %collective-permute-start) | collective-permute-done | bytes 5505056 | tf_op jit(solution)/shard_map/ppermute | solution.py:33
  173.1 39.5 %conditional.1 = (f32[128,3,2,3584]{3,0,2,1:T(8,128)S(1)}, f32[128,3,2,3584]{3,0,2,1:T(8,128)S(1)}, f32[128,3,2,512]{3,0,2,1:T(8,128)}, f32[128,3,2,512]{3,0,2,1:T(8,128)}, f32[128,3,2,512]{3,0,2,1:T(8,128)S(1)}) conditional(s32[]{:T(128)} %convert_element_type.59, (bf16[128,3,2,3584]{3,2,1,0:T(2,128)(2,1)}, bf16[512,3584]{1,0:T(8,128)(2,1)}, ...), branch_computations={%region_4.5_spmd, %region_5.6_spmd} | conditional | flops 14099152896 | bytes 127664304 | solution.py:61
  181.9 8.2 %fusion.29 = (f32[128,3,2,512]{3,0,2,1:T(8,128)}, f32[128,3,2,512]{3,0,2,1:T(8,128)S(1)}) fusion(bf16[3584,512]{1,0:T(8,128)(2,1)} %get-tuple-element.69, bf16[128,3,2,3584]{3,2,1,0:T(2,128)(2,1)} %get-tuple-element.115), kind=kOutput, calls=%fused_computation.41 | convolution fusion | flops 2820145152 | bytes 12320768 | tf_op jit(solution)/shard_map/cond/branch_1_fun/ejqc,cf->ejqf/dot_general | solution.py:40
  190.1 5.1 %fusion.18 = f32[128,3,2,512]{3,0,2,1:T(8,128)S(1)} fusion(bf16[128,3,2,3584]{3,2,1,0:T(2,128)(2,1)} %get-tuple-element.115, bf16[3584,512]{1,0:T(8,128)(2,1)S(1)} %copy-done.4), kind=kOutput, calls=%fused_computation.27 | convolution fusion | flops 2818572288 | bytes 10747904 | tf_op jit(solution)/shard_map/cond/branch_1_fun/ejqc,cf->ejqf/dot_general | solution.py:43
  195.2 7.4 %fusion.16 = f32[128,3,2,512]{3,0,2,1:T(8,128)} fusion(bf16[128,3,2,3584]{3,2,1,0:T(2,128)(2,1)} %get-tuple-element.113, bf16[512,3584]{1,0:T(8,128)(2,1)S(1)} %copy-done.12), kind=kOutput, calls=%fused_computation.25 | convolution fusion | flops 2818572288 | bytes 10747904 | tf_op jit(solution)/shard_map/cond/branch_1_fun/ejqc,fc->ejqf/dot_general | solution.py:44
  202.6 4.9 %fusion.22 = f32[128,3,2,3584]{3,0,2,1:T(8,128)S(1)} fusion(bf16[3584,512]{1,0:T(8,128)(2,1)S(1)} %copy-done.2, f32[128,3,2,512]{3,0,2,1:T(8,128)S(1)} %get-tuple-element.121, f32[128,3,2,512]{3,0,2,1:T(8,128)} %fusion.16, f32[128,3,2,512]{3,0,2,1:T(8,128)S(1)} %fusion.18), kind=kOutput, calls=%fused_computation.31 | convolution fusion | flops 2822504448 | bytes 19398656 | tf_op jit(solution)/shard_map/cond/branch_1_fun/ejqf,cf->ejqc/dot_general | solution.py:54
  207.5 5.1 %fusion.26 = f32[128,3,2,3584]{3,0,2,1:T(8,128)S(1)} fusion(bf16[3584,512]{1,0:T(8,128)(2,1)S(1)} %copy-done.4, f32[128,3,2,512]{3,0,2,1:T(8,128)} %fusion.16, f32[128,3,2,512]{3,0,2,1:T(8,128)} %get-tuple-element.142), kind=kOutput, calls=%fused_computation.35 | convolution fusion | flops 2819358720 | bytes 17825792 | tf_op jit(solution)/shard_map/cond/branch_1_fun/ejqf,cf->ejqc/dot_general | solution.py:56
  213.9 2.4 copy-done
  216.3 1.8 dynamic-slice_convert_fusion
  218.1 2.2 multiply_reduce_fusion
  221.1 2.4 collective-permute-done.2
  223.8 3.3 add_convert_fusion
  227.3 4.6 %copy.141 = bf16[128,3,2,1920]{3,2,1,0:T(2,128)(2,1)} copy(bf16[128,3,2,1920]{3,0,2,1:T(8,128)(2,1)S(1)} %fusion.33) | data formatting | bytes 5898240 | tf_op jit(solution)/shard_map/concatenate | solution.py:74
  232.0 8.4 %all-to-all-start.1 = ((bf16[128,3,2,1920]{3,2,1,0:T(2,128)(2,1)}), bf16[128,3,2,1920]{3,2,1,0:T(2,128)(2,1)S(1)}, u32[]{:S(2)}, u32[]{:S(2)}) async-start(bf16[128,3,2,1920]{3,2,1,0:T(2,128)(2,1)} %copy.141), calls=%async_computation.1 | async-start | bytes 5898240 | tf_op jit(solution)/shard_map/all_to_all | solution.py:75
  241.0 69.8 %all-to-all-done.1 = bf16[128,3,2,1920]{3,2,1,0:T(2,128)(2,1)S(1)} async-done(((bf16[128,3,2,1920]{3,2,1,0:T(2,128)(2,1)}), bf16[128,3,2,1920]{3,2,1,0:T(2,128)(2,1)S(1)}, u32[]{:S(2)}, u32[]{:S(2)}) %all-to-all-start.1) | async-done | bytes 2949152 | tf_op jit(solution)/shard_map/all_to_all | solution.py:75
  310.7 1.9 gather_fusion.1
  312.7 2.7 gather_fusion.2
  316.2 2.6 gather_fusion.3
  319.6 2.6 gather_fusion.4
  323.7 2.5 add_convert_fusion.1
  (67 shorter events, 9.6 us)
Async XLA Ops:
  0.6 5.7 %copy-start.7 = (bf16[128,3584]{1,0:T(8,128)(2,1)S(1)}, bf16[128,3584]{1,0:T(8,128)(2,1)}, u32[]{:S(2)}) copy-start(bf16[128,3584]{1,0:T(8,128)(2,1)} %param.11) | copy-start | bytes 2752516
  0.6 5.7 %copy-start.8 = (bf16[128,3584]{1,0:T(8,128)(2,1)S(1)}, bf16[128,3584]{1,0:T(8,128)(2,1)}, u32[]{:S(2)}) copy-start(bf16[128,3584]{1,0:T(8,128)(2,1)} %param.12) | copy-start | bytes 2752516
  163.7 9.4 %collective-permute-start = (bf16[128,3,2,3584]{3,2,1,0:T(2,128)(2,1)}, bf16[128,3,2,3584]{3,2,1,0:T(2,128)(2,1)}, u32[]{:S(2)}, u32[]{:S(2)}) collective-permute-start(bf16[128,3,2,3584]{3,2,1,0:T(2,128)(2,1)} %all_to_all.10), channel_id=1, source_target_pairs={{0,1},{1,0},{2,3},{3,2},{4,5},{5,4},{6,7},{7,6},{8,9},{9,8},{10,11... | collective-permute-start | bytes 16515080 | tf_op jit(solution)/shard_map/ppermute | solution.py:33
  181.8 8.2 %copy-start.4 = (bf16[3584,512]{1,0:T(8,128)(2,1)S(1)}, bf16[3584,512]{1,0:T(8,128)(2,1)}, u32[]{:S(2)}) copy-start(bf16[3584,512]{1,0:T(8,128)(2,1)} %get-tuple-element.68) | copy-start | bytes 11010052 | tf_op jit(solution)/shard_map/cond
  190.0 5.1 %copy-start.12 = (bf16[512,3584]{1,0:T(8,128)(2,1)S(1)}, bf16[512,3584]{1,0:T(8,128)(2,1)}, u32[]{:S(2)}) copy-start(bf16[512,3584]{1,0:T(8,128)(2,1)} %get-tuple-element.66) | copy-start | bytes 11010052 | tf_op jit(solution)/shard_map/cond
  195.2 7.4 %copy-start.5 = (f32[128,3,2,512]{3,0,2,1:T(8,128)}, f32[128,3,2,512]{3,0,2,1:T(8,128)S(1)}, u32[]{:S(2)}) copy-start(f32[128,3,2,512]{3,0,2,1:T(8,128)S(1)} %fusion.18) | copy-start | bytes 4718596 | tf_op jit(solution)/shard_map/cond
  195.2 7.4 %copy-start.2 = (bf16[3584,512]{1,0:T(8,128)(2,1)S(1)}, bf16[3584,512]{1,0:T(8,128)(2,1)}, u32[]{:S(2)}) copy-start(bf16[3584,512]{1,0:T(8,128)(2,1)} %get-tuple-element.69) | copy-start | bytes 11010052 | tf_op jit(solution)/shard_map/cond
  207.5 5.1 %copy-start.6 = (f32[128,3,2,512]{3,0,2,1:T(8,128)S(1)}, f32[128,3,2,512]{3,0,2,1:T(8,128)}, u32[]{:S(2)}) copy-start(f32[128,3,2,512]{3,0,2,1:T(8,128)} %copy-done.5) | copy-start | bytes 4718596 | tf_op jit(solution)/shard_map/cond
  213.9 2.4 copy-start
  218.1 5.6 %collective-permute-start.1 = (bf16[128,3,2,1792]{3,0,2,1:T(8,128)(2,1)}, bf16[128,3,2,1792]{3,0,2,1:T(8,128)(2,1)}, u32[]{:S(2)}, u32[]{:S(2)}) collective-permute-start(bf16[128,3,2,1792]{3,0,2,1:T(8,128)(2,1)} %dynamic-slice_convert_fusion), channel_id=1, source_target_pairs={{0,1},{1,0},{2,3},{3,2},{4,5},{5,4},{6,7},{7,6},{8,9},{9,8},{10,11... | collective-permute-start | bytes 8257544 | tf_op jit(solution)/shard_map/ppermute | solution.py:68
  220.3 3.3 %collective-permute-start.2 = (f32[128,3,2]{0,2,1:T(2,128)S(1)}, f32[128,3,2]{0,2,1:T(2,128)S(1)}, u32[]{:S(2)}, u32[]{:S(2)}) collective-permute-start(f32[128,3,2]{0,2,1:T(2,128)S(1)} %multiply_reduce_fusion), channel_id=1, source_target_pairs={{0,1},{1,0},{2,3},{3,2},{4,5},{5,4},{6,7},{7,6},{8,9},{9,8},{10,11... | collective-permute-start | bytes 9224 | tf_op jit(solution)/shard_map/ppermute | solution.py:72
  232.0 8.9 %copy-start.10 = (f32[128,4]{0,1:T(4,128)S(1)}, f32[128,4]{0,1:T(4,128)}, u32[]{:S(2)}) copy-start(f32[128,4]{0,1:T(4,128)} %param.14) | copy-start | bytes 6148
  232.0 9.0 %copy-start.9 = (s32[128,4]{0,1:T(4,128)S(1)}, s32[128,4]{0,1:T(4,128)}, u32[]{:S(2)}) copy-start(s32[128,4]{0,1:T(4,128)} %param.13) | copy-start | bytes 6148
  232.0 78.8 %all-to-all-start.1 = ((bf16[128,3,2,1920]{3,2,1,0:T(2,128)(2,1)}), bf16[128,3,2,1920]{3,2,1,0:T(2,128)(2,1)S(1)}, u32[]{:S(2)}, u32[]{:S(2)}) async-start(bf16[128,3,2,1920]{3,2,1,0:T(2,128)(2,1)} %copy.141), calls=%async_computation.1 | async-start | bytes 5898240 | tf_op jit(solution)/shard_map/all_to_all | solution.py:75

commit v7 on v5

--- a/solution.py
+++ b/solution.py
@@ -60,7 +60,7 @@
     grad_share = (
         own_half.astype(jnp.bfloat16).astype(jnp.float32) + got_half.astype(jnp.float32)
     ).astype(jnp.bfloat16)
-    score_full = lax.psum(score_part, "hid").astype(jnp.bfloat16)
+    score_full = (score_part + lax.ppermute(score_part, "hid", swap)).astype(jnp.bfloat16)
     score_cols = jnp.zeros(quad + (128,), jnp.bfloat16).at[..., 0].set(score_full)
     back_send = jnp.concatenate([grad_share, score_cols], axis=3)
     back = lax.all_to_all(back_send, "expert", split_axis=0, concat_axis=0, tiled=True)

time: 315 us -> 315 us (level)
  blocking collectives: 146 us -> 140 us
  waiting for transfers between devices: 79.3 us -> 84.1 us
    psum x1 -> x0, blocking collectives: 5.2 us -> none  [body(): score_full = lax.psum(score_part, 'hid').astype(jnp.bfloat16)]
    ppermute x0 -> x1, waiting for transfers between devices: none -> 4.8 us  [body(): lax.ppermute(score_part, 'hid', swap)]
  transfers between devices with their start and end apart: 3 -> 4, of which waited for: 2 -> 3; matrix products, arithmetic and copies ran while one was open for 0% -> 0% of each run, Pallas kernels for 0% -> 0%
where the time goes in v7:
time: 315 us; the launch traced here: 314 us
  blocking collectives  140 us (44%)
  waiting for transfers between devices  84.1 us (27%)
  local copies, waits for them, and re-layouts  42.4 us (13%)
  matrix products  19.8 us (6%)
  other arithmetic  18.2 us (6%)
  starting transfers between devices  8.5 us (3%)
    all_to_all x1, blocking collectives, body(): lax.all_to_all(send, 'expert', split_axis=0, concat_axis=0, tiled=True)  140 us
    all_to_all x1, waiting for transfers between devices, body(): lax.all_to_all(back_send, 'expert', split_axis=0, concat_axis=0, tiled=True)  69.9 us
    gather x2, local copies, waits for them, and re-layouts, body(): send = source[slot_token.reshape(quad)]  16.8 us
    select_n x1, other arithmetic, body(): rows_x = jnp.where(first, recv, other)  11 us
    gather x4, local copies, waits for them, and re-layouts, body(): row = back[route_ids[:, k], route_slot[:, k] // 2, route_slot[:, k] % 2]  9.81 us
    ppermute x1, waiting for transfers between devices, body(): other = lax.ppermute(recv, 'hid', swap)  9.37 us
    all_to_all x1, starting transfers between devices, body(): lax.all_to_all(back_send, 'expert', split_axis=0, concat_axis=0, tiled=True)  7.98 us
    dot_general x1, matrix products, body(): jnp.einsum('ejqf,cf->ejqc', grad_up_pre, up_mat, preferred_element_type=j...  6.91 us
  transfers between devices with their start and end apart: 4, of which 3 were waited for; matrix products, arithmetic and copies ran while one was open for 0% of the time, Pallas kernels for 0%

profile of v7, /device:TPU:2, one launch (start us, length us, event | category | flops | bytes accessed | tf_op | source)
XLA Modules:
  0.0 314.3 jit_solution(5456625163234797048)
XLA Ops:
  0.6 0.9 copy.114
  3.4 2.4 scatter_custom_fusion
  6.4 5.4 %gather_fusion = bf16[768,3584]{1,0:T(8,128)(2,1)} fusion(bf16[128,3584]{1,0:T(8,128)(2,1)S(1)} %broadcast_select_fusion.2, s32[1024]{0:T(1024)S(1)} %pad_clamp_fusion), kind=kCustom, calls=%fused_computation | custom fusion | bytes 11013120 | tf_op jit(solution)/shard_map/gather | solution.py:30
  11.9 11.4 %reshape.128 = bf16[128,3,2,3584]{3,2,1,0:T(2,128)(2,1)} reshape(bf16[768,3584]{1,0:T(8,128)(2,1)} %gather_fusion) | data formatting | bytes 11010048 | tf_op jit(solution)/shard_map/gather | solution.py:30
  23.3 140.4 %all_to_all.10 = bf16[128,3,2,3584]{3,2,1,0:T(2,128)(2,1)} all-to-all(bf16[128,3,2,3584]{3,2,1,0:T(2,128)(2,1)} %reshape.128), channel_id=1, replica_groups=mesh['expert'=128,'hid'=2] {'expert'}, dimensions={0} | all-to-all | bytes 11010048 | tf_op jit(solution)/shard_map/all_to_all | solution.py:31
  163.7 9.4 %collective-permute-done = bf16[128,3,2,3584]{3,2,1,0:T(2,128)(2,1)} collective-permute-done((bf16[128,3,2,3584]{3,2,1,0:T(2,128)(2,1)}, bf16[128,3,2,3584]{3,2,1,0:T(2,128)(2,1)}, u32[]{:S(2)}, u32[]{:S(2)}) %collective-permute-start) | collective-permute-done | bytes 5505056 | tf_op jit(solution)/shard_map/ppermute | solution.py:33
  173.1 11.0 %broadcast_select_fusion = (bf16[128,3,2,3584]{3,2,1,0:T(2,128)(2,1)S(1)}, bf16[128,3,2,3584]{3,2,1,0:T(2,128)(2,1)S(1)}) fusion(bf16[128,3,2,3584]{3,2,1,0:T(2,128)(2,1)} %all_to_all.10, bf16[128,3,2,3584]{3,2,1,0:T(2,128)(2,1)} %collective-permute-done, pred[]{:T(512)S(6)} %eq.34), kind=kLoop, calls=%fused_computation.6 | loop fusion | flops 5505024 | bytes 22020096 | tf_op jit(solution)/shard_map/jit(_where)/select_n | solution.py:35
  184.1 3.0 fusion.3
  187.2 3.0 fusion.5
  190.2 3.4 %multiply_reduce_fusion = (f32[128,3,2]{0,2,1:T(2,128)S(1)}, f32[128,3,2,512]{3,0,2,1:T(8,128)S(1)}) fusion(f32[128,3,2,512]{3,0,2,1:T(8,128)S(1)} %fusion.5, f32[128,3,2,512]{3,0,2,1:T(8,128)S(1)} %fusion.3, bf16[1,512,3584]{2,1,0:T(8,128)(2,1)S(1)} %copy-done.6, bf16[128,3,2,3584]{3,2,1,0:T(2,128)(2,1)S(1)} %get-tuple-element.21), kind=kOutput, calls=%fused_computation.27 | convolution fusion | flops 2821324032 | bytes 13896704 | tf_op jit(solution)/shard_map/ejqc,fc->ejqf/dot_general | solution.py:42
  193.5 3.5 %fusion.7 = f32[128,3,2,3584]{3,0,2,1:T(8,128)S(1)} fusion(bf16[1,3584,512]{2,1,0:T(8,128)(2,1)S(1)} %copy-done, f32[128,3,2,512]{3,0,2,1:T(8,128)S(1)} %fusion.3, f32[128,3,2,512]{3,0,2,1:T(8,128)S(1)} %get-tuple-element.35, f32[128,3,2,512]{3,0,2,1:T(8,128)S(1)} %fusion.5), kind=kOutput, calls=%fused_computation.20 | convolution fusion | flops 2822504448 | bytes 19398656 | tf_op jit(solution)/shard_map/ejqf,cf->ejqc/dot_general | solution.py:52
  197.1 6.9 %convolution_add_fusion = bf16[128,3,2,3584]{3,0,2,1:T(8,128)(2,1)} fusion(f32[128,3,2,3584]{3,0,2,1:T(8,128)S(1)} %fusion.7, bf16[1,3584,512]{2,1,0:T(8,128)(2,1)} %param.14, f32[128,3,2,512]{3,0,2,1:T(8,128)S(1)} %get-tuple-element.35, f32[128,3,2,512]{3,0,2,1:T(8,128)S(1)} %fusion.3), kind=kOutput, calls=%fused_computation.8 | convolution fusion | flops 2826436608 | bytes 23330816 | tf_op jit(solution)/shard_map/ejqf,cf->ejqc/dot_general | solution.py:54
  204.0 3.5 %dynamic-slice_convert_fusion = bf16[128,3,2,1792]{3,0,2,1:T(8,128)(2,1)} fusion(bf16[128,3,2,3584]{3,0,2,1:T(8,128)(2,1)} %convolution_add_fusion, s32[]{:T(128)S(6)} %select_n.149), kind=kLoop, calls=%fused_computation.14 | loop fusion | bytes 5505028 | tf_op jit(solution)/shard_map/convert_element_type | solution.py:58
  208.0 4.8 %collective-permute-done.2 = f32[128,3,2]{0,2,1:T(2,128)S(1)} collective-permute-done((f32[128,3,2]{0,2,1:T(2,128)S(1)}, f32[128,3,2]{0,2,1:T(2,128)S(1)}, u32[]{:S(2)}, u32[]{:S(2)}) %collective-permute-start.2) | collective-permute-done | bytes 3104 | tf_op jit(solution)/shard_map/ppermute | solution.py:63
  213.0 2.4 add_convert_fusion
  215.7 4.6 %copy.122 = bf16[128,3,2,1920]{3,2,1,0:T(2,128)(2,1)} copy(bf16[128,3,2,1920]{3,0,2,1:T(8,128)(2,1)S(1)} %fusion.13) | data formatting | bytes 5898240 | tf_op jit(solution)/shard_map/concatenate | solution.py:65
  220.4 8.0 %all-to-all-start.1 = ((bf16[128,3,2,1920]{3,2,1,0:T(2,128)(2,1)}), bf16[128,3,2,1920]{3,2,1,0:T(2,128)(2,1)S(1)}, u32[]{:S(2)}, u32[]{:S(2)}) async-start(bf16[128,3,2,1920]{3,2,1,0:T(2,128)(2,1)} %copy.122), calls=%async_computation.1 | async-start | bytes 5898240 | tf_op jit(solution)/shard_map/all_to_all | solution.py:66
  229.0 69.9 %all-to-all-done.1 = bf16[128,3,2,1920]{3,2,1,0:T(2,128)(2,1)S(1)} async-done(((bf16[128,3,2,1920]{3,2,1,0:T(2,128)(2,1)}), bf16[128,3,2,1920]{3,2,1,0:T(2,128)(2,1)S(1)}, u32[]{:S(2)}, u32[]{:S(2)}) %all-to-all-start.1) | async-done | bytes 2949152 | tf_op jit(solution)/shard_map/all_to_all | solution.py:66
  298.8 1.9 gather_fusion.1
  300.8 2.7 gather_fusion.2
  303.5 0.8 slice.140
  304.3 2.7 gather_fusion.3
  307.8 2.6 gather_fusion.4
  311.9 2.5 add_convert_fusion.1
  (59 shorter events, 6.3 us)
Async XLA Ops:
  0.6 5.7 %copy-start.3 = (bf16[128,3584]{1,0:T(8,128)(2,1)S(1)}, bf16[128,3584]{1,0:T(8,128)(2,1)}, u32[]{:S(2)}) copy-start(bf16[128,3584]{1,0:T(8,128)(2,1)} %param.10) | copy-start | bytes 2752516
  0.6 5.7 %copy-start.2 = (bf16[128,3584]{1,0:T(8,128)(2,1)S(1)}, bf16[128,3584]{1,0:T(8,128)(2,1)}, u32[]{:S(2)}) copy-start(bf16[128,3584]{1,0:T(8,128)(2,1)} %param.9) | copy-start | bytes 2752516
  163.7 9.4 %collective-permute-start = (bf16[128,3,2,3584]{3,2,1,0:T(2,128)(2,1)}, bf16[128,3,2,3584]{3,2,1,0:T(2,128)(2,1)}, u32[]{:S(2)}, u32[]{:S(2)}) collective-permute-start(bf16[128,3,2,3584]{3,2,1,0:T(2,128)(2,1)} %all_to_all.10), channel_id=1, source_target_pairs={{0,1},{1,0},{2,3},{3,2},{4,5},{5,4},{6,7},{7,6},{8,9},{9,8},{10,11... | collective-permute-start | bytes 16515080 | tf_op jit(solution)/shard_map/ppermute | solution.py:33
  163.7 20.4 %copy-start = (bf16[1,3584,512]{2,1,0:T(8,128)(2,1)S(1)}, bf16[1,3584,512]{2,1,0:T(8,128)(2,1)}, u32[]{:S(2)}) copy-start(bf16[1,3584,512]{2,1,0:T(8,128)(2,1)} %param.13) | copy-start | bytes 11010052
  184.1 3.0 copy-start.1
  187.2 3.0 copy-start.6
  207.5 5.5 %collective-permute-start.1 = (bf16[128,3,2,1792]{3,0,2,1:T(8,128)(2,1)}, bf16[128,3,2,1792]{3,0,2,1:T(8,128)(2,1)S(1)}, u32[]{:S(2)}, u32[]{:S(2)}) collective-permute-start(bf16[128,3,2,1792]{3,0,2,1:T(8,128)(2,1)} %dynamic-slice_convert_fusion), channel_id=1, source_target_pairs={{0,1},{1,0},{2,3},{3,2},{4,5},{5,4},{6,7},{7,6},{8,9},{9,8},{10,11... | collective-permute-start | bytes 8257544 | tf_op jit(solution)/shard_map/ppermute | solution.py:59
  207.6 5.1 %collective-permute-start.2 = (f32[128,3,2]{0,2,1:T(2,128)S(1)}, f32[128,3,2]{0,2,1:T(2,128)S(1)}, u32[]{:S(2)}, u32[]{:S(2)}) collective-permute-start(f32[128,3,2]{0,2,1:T(2,128)S(1)} %get-tuple-element.34), channel_id=1, source_target_pairs={{0,1},{1,0},{2,3},{3,2},{4,5},{5,4},{6,7},{7,6},{8,9},{9,8},{10,11... | collective-permute-start | bytes 9224 | tf_op jit(solution)/shard_map/ppermute | solution.py:63
  220.3 8.5 %copy-start.5 = (f32[128,4]{0,1:T(4,128)S(1)}, f32[128,4]{0,1:T(4,128)}, u32[]{:S(2)}) copy-start(f32[128,4]{0,1:T(4,128)} %param.12) | copy-start | bytes 6148
  220.4 8.6 %copy-start.4 = (s32[128,4]{0,1:T(4,128)S(1)}, s32[128,4]{0,1:T(4,128)}, u32[]{:S(2)}) copy-start(s32[128,4]{0,1:T(4,128)} %param.11) | copy-start | bytes 6148
  220.4 78.5 %all-to-all-start.1 = ((bf16[128,3,2,1920]{3,2,1,0:T(2,128)(2,1)}), bf16[128,3,2,1920]{3,2,1,0:T(2,128)(2,1)S(1)}, u32[]{:S(2)}, u32[]{:S(2)}) async-start(bf16[128,3,2,1920]{3,2,1,0:T(2,128)(2,1)} %copy.122), calls=%async_computation.1 | async-start | bytes 5898240 | tf_op jit(solution)/shard_map/all_to_all | solution.py:66

commit v8 on v7

--- a/solution.py
+++ b/solution.py
@@ -27,7 +27,12 @@
     slot_token = slot_pair // top_count
     source = jnp.where(hid_idx == 0, tokens, out_grad)
     quad = (expert_count, capacity // 2, 2)
-    send = source[slot_token.reshape(quad)]
+    pick = (
+        slot_token.reshape(quad)[..., None] == jnp.arange(tok_rows, dtype=jnp.int32)
+    ).astype(jnp.bfloat16)
+    send = jnp.einsum(
+        "ejqt,tc->ejqc", pick, source, preferred_element_type=jnp.float32
+    ).astype(jnp.bfloat16)
     recv = lax.all_to_all(send, "expert", split_axis=0, concat_axis=0, tiled=True)
     swap = [(0, 1), (1, 0)]
     other = lax.ppermute(recv, "hid", swap)

time: 315 us -> 333 us (1.057)
  local copies, waits for them, and re-layouts: 42.4 us -> 58.2 us
    convert_element_type x0 -> x1, local copies, waits for them, and re-layouts: none -> 32.7 us  [body(): send = jnp.einsum('ejqt,tc->ejqc', pick, source, preferred_element_type=j...]
    gather x2 -> x0, local copies, waits for them, and re-layouts: 16.8 us -> none  [body(): send = source[slot_token.reshape(quad)]]
where the time goes in v8:
time: 333 us
  blocking collectives  140 us (42%)
  waiting for transfers between devices  84 us (25%)
  local copies, waits for them, and re-layouts  58.2 us (17%)
  matrix products  22.8 us (7%)
  other arithmetic  18.1 us (5%)
  starting transfers between devices  8.52 us (3%)
    all_to_all x1, blocking collectives, body(): lax.all_to_all(send, 'expert', split_axis=0, concat_axis=0, tiled=True)  140 us
    all_to_all x1, waiting for transfers between devices, body(): lax.all_to_all(back_send, 'expert', split_axis=0, concat_axis=0, tiled=True)  69.9 us
    convert_element_type x1, local copies, waits for them, and re-layouts, body(): send = jnp.einsum('ejqt,tc->ejqc', pick, source, preferred_element_type=j...  32.7 us
    select_n x1, other arithmetic, body(): rows_x = jnp.where(first, recv, other)  11 us
    gather x4, local copies, waits for them, and re-layouts, body(): row = back[route_ids[:, k], route_slot[:, k] // 2, route_slot[:, k] % 2]  9.81 us
    ppermute x1, waiting for transfers between devices, body(): other = lax.ppermute(recv, 'hid', swap)  9.37 us
    all_to_all x1, starting transfers between devices, body(): lax.all_to_all(back_send, 'expert', split_axis=0, concat_axis=0, tiled=True)  8 us
    dot_general x1, matrix products, body(): jnp.einsum('ejqf,cf->ejqc', grad_up_pre, up_mat, preferred_element_type=j...  6.9 us
  transfers between devices with their start and end apart: 4, of which 3 were waited for; matrix products, arithmetic and copies ran while one was open for 0% of the time, Pallas kernels for 0%

profile of v8, /device:TPU:2, one launch (start us, length us, event | category | flops | bytes accessed | tf_op | source)
XLA Modules:
  0.0 332.7 jit_solution(15802809395035380126)
XLA Ops:
  0.6 0.9 copy.115
  3.4 2.4 scatter_custom_fusion
  6.2 1.7 convolution_convert_fusion
  7.8 32.7 %copy.120 = bf16[128,3,2,3584]{3,2,1,0:T(2,128)(2,1)S(1)} copy(bf16[128,3,2,3584]{3,0,2,1:T(8,128)(2,1)S(1)} %convolution_convert_fusion) | data formatting | bytes 11010048 | tf_op jit(solution)/shard_map/convert_element_type | solution.py:35
  40.5 140.2 %all_to_all.10 = bf16[128,3,2,3584]{3,2,1,0:T(2,128)(2,1)} all-to-all(bf16[128,3,2,3584]{3,2,1,0:T(2,128)(2,1)S(1)} %copy.120), channel_id=1, replica_groups=mesh['expert'=128,'hid'=2] {'expert'}, dimensions={0} | all-to-all | bytes 11010048 | tf_op jit(solution)/shard_map/all_to_all | solution.py:36
  180.7 9.4 %collective-permute-done = bf16[128,3,2,3584]{3,2,1,0:T(2,128)(2,1)} collective-permute-done((bf16[128,3,2,3584]{3,2,1,0:T(2,128)(2,1)}, bf16[128,3,2,3584]{3,2,1,0:T(2,128)(2,1)}, u32[]{:S(2)}, u32[]{:S(2)}) %collective-permute-start) | collective-permute-done | bytes 5505056 | tf_op jit(solution)/shard_map/ppermute | solution.py:38
  190.1 11.0 %broadcast_select_fusion = (bf16[128,3,2,3584]{3,2,1,0:T(2,128)(2,1)S(1)}, bf16[128,3,2,3584]{3,2,1,0:T(2,128)(2,1)S(1)}) fusion(bf16[128,3,2,3584]{3,2,1,0:T(2,128)(2,1)} %all_to_all.10, bf16[128,3,2,3584]{3,2,1,0:T(2,128)(2,1)} %collective-permute-done, pred[]{:T(512)S(6)} %eq.49), kind=kLoop, calls=%fused_computation.5 | loop fusion | flops 5505024 | bytes 22020096 | tf_op jit(solution)/shard_map/jit(_where)/select_n | solution.py:40
  201.1 3.0 fusion.3
  204.2 3.0 fusion.5
  207.2 3.3 multiply_reduce_fusion
  210.5 4.9 %fusion.7 = f32[128,3,2,3584]{3,0,2,1:T(8,128)S(1)} fusion(bf16[1,3584,512]{2,1,0:T(8,128)(2,1)S(1)} %copy-done, f32[128,3,2,512]{3,0,2,1:T(8,128)S(1)} %fusion.3, f32[128,3,2,512]{3,0,2,1:T(8,128)S(1)} %get-tuple-element.35, f32[128,3,2,512]{3,0,2,1:T(8,128)} %copy-done.2), kind=kOutput, calls=%fused_computation.20 | convolution fusion | flops 2822504448 | bytes 19398656 | tf_op jit(solution)/shard_map/ejqf,cf->ejqc/dot_general | solution.py:57
  215.4 6.9 %convolution_add_fusion = bf16[128,3,2,3584]{3,0,2,1:T(8,128)(2,1)} fusion(f32[128,3,2,3584]{3,0,2,1:T(8,128)S(1)} %fusion.7, bf16[1,3584,512]{2,1,0:T(8,128)(2,1)} %param.14, f32[128,3,2,512]{3,0,2,1:T(8,128)S(1)} %get-tuple-element.35, f32[128,3,2,512]{3,0,2,1:T(8,128)S(1)} %fusion.3), kind=kOutput, calls=%fused_computation.7 | convolution fusion | flops 2826436608 | bytes 23330816 | tf_op jit(solution)/shard_map/ejqf,cf->ejqc/dot_general | solution.py:59
  222.3 3.5 %dynamic-slice_convert_fusion = bf16[128,3,2,1792]{3,0,2,1:T(8,128)(2,1)} fusion(bf16[128,3,2,3584]{3,0,2,1:T(8,128)(2,1)} %convolution_add_fusion, s32[]{:T(128)S(6)} %select_n.138), kind=kLoop, calls=%fused_computation.14 | loop fusion | bytes 5505028 | tf_op jit(solution)/shard_map/convert_element_type | solution.py:63
  226.3 4.8 %collective-permute-done.2 = f32[128,3,2]{0,2,1:T(2,128)S(1)} collective-permute-done((f32[128,3,2]{0,2,1:T(2,128)S(1)}, f32[128,3,2]{0,2,1:T(2,128)S(1)}, u32[]{:S(2)}, u32[]{:S(2)}) %collective-permute-start.2) | collective-permute-done | bytes 3104 | tf_op jit(solution)/shard_map/ppermute | solution.py:68
  231.3 2.4 add_convert_fusion
  234.1 4.6 %copy.125 = bf16[128,3,2,1920]{3,2,1,0:T(2,128)(2,1)} copy(bf16[128,3,2,1920]{3,0,2,1:T(8,128)(2,1)S(1)} %fusion.13) | data formatting | bytes 5898240 | tf_op jit(solution)/shard_map/concatenate | solution.py:70
  238.7 8.0 %all-to-all-start.1 = ((bf16[128,3,2,1920]{3,2,1,0:T(2,128)(2,1)}), bf16[128,3,2,1920]{3,2,1,0:T(2,128)(2,1)S(1)}, u32[]{:S(2)}, u32[]{:S(2)}) async-start(bf16[128,3,2,1920]{3,2,1,0:T(2,128)(2,1)} %copy.125), calls=%async_computation.1 | async-start | bytes 5898240 | tf_op jit(solution)/shard_map/all_to_all | solution.py:71
  247.3 69.9 %all-to-all-done.1 = bf16[128,3,2,1920]{3,2,1,0:T(2,128)(2,1)S(1)} async-done(((bf16[128,3,2,1920]{3,2,1,0:T(2,128)(2,1)}), bf16[128,3,2,1920]{3,2,1,0:T(2,128)(2,1)S(1)}, u32[]{:S(2)}, u32[]{:S(2)}) %all-to-all-start.1) | async-done | bytes 2949152 | tf_op jit(solution)/shard_map/all_to_all | solution.py:71
  317.2 1.9 gather_fusion
  319.1 2.7 gather_fusion.1
  321.8 0.8 slice.138
  322.6 2.6 gather_fusion.2
  326.1 2.6 gather_fusion.3
  330.2 2.5 add_convert_fusion.1
  (58 shorter events, 6.1 us)
Async XLA Ops:
  0.6 5.5 %copy-start.4 = (bf16[128,3584]{1,0:T(8,128)(2,1)S(1)}, bf16[128,3584]{1,0:T(8,128)(2,1)}, u32[]{:S(2)}) copy-start(bf16[128,3584]{1,0:T(8,128)(2,1)} %param.10) | copy-start | bytes 2752516
  0.6 5.5 %copy-start.3 = (bf16[128,3584]{1,0:T(8,128)(2,1)S(1)}, bf16[128,3584]{1,0:T(8,128)(2,1)}, u32[]{:S(2)}) copy-start(bf16[128,3584]{1,0:T(8,128)(2,1)} %param.9) | copy-start | bytes 2752516
  180.7 9.4 %collective-permute-start = (bf16[128,3,2,3584]{3,2,1,0:T(2,128)(2,1)}, bf16[128,3,2,3584]{3,2,1,0:T(2,128)(2,1)}, u32[]{:S(2)}, u32[]{:S(2)}) collective-permute-start(bf16[128,3,2,3584]{3,2,1,0:T(2,128)(2,1)} %all_to_all.10), channel_id=1, source_target_pairs={{0,1},{1,0},{2,3},{3,2},{4,5},{5,4},{6,7},{7,6},{8,9},{9,8},{10,11... | collective-permute-start | bytes 16515080 | tf_op jit(solution)/shard_map/ppermute | solution.py:38
  180.7 20.4 %copy-start = (bf16[1,3584,512]{2,1,0:T(8,128)(2,1)S(1)}, bf16[1,3584,512]{2,1,0:T(8,128)(2,1)}, u32[]{:S(2)}) copy-start(bf16[1,3584,512]{2,1,0:T(8,128)(2,1)} %param.13) | copy-start | bytes 11010052
  201.1 3.0 copy-start.1
  204.1 3.0 copy-start.7
  207.2 3.3 copy-start.2
  225.8 5.5 %collective-permute-start.1 = (bf16[128,3,2,1792]{3,0,2,1:T(8,128)(2,1)}, bf16[128,3,2,1792]{3,0,2,1:T(8,128)(2,1)S(1)}, u32[]{:S(2)}, u32[]{:S(2)}) collective-permute-start(bf16[128,3,2,1792]{3,0,2,1:T(8,128)(2,1)} %dynamic-slice_convert_fusion), channel_id=1, source_target_pairs={{0,1},{1,0},{2,3},{3,2},{4,5},{5,4},{6,7},{7,6},{8,9},{9,8},{10,11... | collective-permute-start | bytes 8257544 | tf_op jit(solution)/shard_map/ppermute | solution.py:64
  225.9 5.2 %collective-permute-start.2 = (f32[128,3,2]{0,2,1:T(2,128)S(1)}, f32[128,3,2]{0,2,1:T(2,128)S(1)}, u32[]{:S(2)}, u32[]{:S(2)}) collective-permute-start(f32[128,3,2]{0,2,1:T(2,128)S(1)} %get-tuple-element.34), channel_id=1, source_target_pairs={{0,1},{1,0},{2,3},{3,2},{4,5},{5,4},{6,7},{7,6},{8,9},{9,8},{10,11... | collective-permute-start | bytes 9224 | tf_op jit(solution)/shard_map/ppermute | solution.py:68
  238.7 8.5 %copy-start.6 = (f32[128,4]{0,1:T(4,128)S(1)}, f32[128,4]{0,1:T(4,128)}, u32[]{:S(2)}) copy-start(f32[128,4]{0,1:T(4,128)} %param.12) | copy-start | bytes 6148
  238.7 8.6 %copy-start.5 = (s32[128,4]{0,1:T(4,128)S(1)}, s32[128,4]{0,1:T(4,128)}, u32[]{:S(2)}) copy-start(s32[128,4]{0,1:T(4,128)} %param.11) | copy-start | bytes 6148
  238.7 78.5 %all-to-all-start.1 = ((bf16[128,3,2,1920]{3,2,1,0:T(2,128)(2,1)}), bf16[128,3,2,1920]{3,2,1,0:T(2,128)(2,1)S(1)}, u32[]{:S(2)}, u32[]{:S(2)}) async-start(bf16[128,3,2,1920]{3,2,1,0:T(2,128)(2,1)} %copy.125), calls=%async_computation.1 | async-start | bytes 5898240 | tf_op jit(solution)/shard_map/all_to_all | solution.py:71

commit v9 on v7

--- a/solution.py
+++ b/solution.py
@@ -32,8 +32,9 @@
     swap = [(0, 1), (1, 0)]
     other = lax.ppermute(recv, "hid", swap)
     first = hid_idx == 0
-    rows_x = jnp.where(first, recv, other)
-    rows_d = jnp.where(first, other, recv)
+    pair_rows = jnp.stack([recv, other])
+    rows_x = lax.dynamic_index_in_dim(pair_rows, hid_idx, axis=0, keepdims=False)
+    rows_d = lax.dynamic_index_in_dim(pair_rows, 1 - hid_idx, axis=0, keepdims=False)
     gate_mat = w_gate[0]
     up_mat = w_up[0]
     down_mat = w_down[0]

time: 315 us -> 334 us (1.060)
  other arithmetic: 18.2 us -> 36.9 us
    another operation x4 -> x5, other arithmetic: 0.26 us -> 29.9 us  [the longest x1 29.7 us: body(): pair_rows = jnp.stack([recv, other])]
    select_n x1 -> x0, other arithmetic: 11 us -> none  [body(): rows_x = jnp.where(first, recv, other)]
where the time goes in v9:
time: 334 us; the launch traced here: 333 us
  blocking collectives  140 us (42%)
  waiting for transfers between devices  84 us (25%)
  local copies, waits for them, and re-layouts  42.4 us (13%)
  other arithmetic  36.9 us (11%)
  matrix products  20 us (6%)
  starting transfers between devices  8.5 us (3%)
    all_to_all x1, blocking collectives, body(): lax.all_to_all(send, 'expert', split_axis=0, concat_axis=0, tiled=True)  140 us
    all_to_all x1, waiting for transfers between devices, body(): lax.all_to_all(back_send, 'expert', split_axis=0, concat_axis=0, tiled=True)  69.9 us
    another operation x1, other arithmetic, body(): pair_rows = jnp.stack([recv, other])  29.7 us
    gather x2, local copies, waits for them, and re-layouts, body(): send = source[slot_token.reshape(quad)]  16.8 us
    gather x4, local copies, waits for them, and re-layouts, body(): row = back[route_ids[:, k], route_slot[:, k] // 2, route_slot[:, k] % 2]  9.81 us
    ppermute x1, waiting for transfers between devices, body(): other = lax.ppermute(recv, 'hid', swap)  9.37 us
    all_to_all x1, starting transfers between devices, body(): lax.all_to_all(back_send, 'expert', split_axis=0, concat_axis=0, tiled=True)  7.98 us
    dot_general x1, matrix products, body(): jnp.einsum('ejqf,cf->ejqc', grad_up_pre, up_mat, preferred_element_type=j...  7.13 us
  transfers between devices with their start and end apart: 4, of which 3 were waited for; matrix products, arithmetic and copies ran while one was open for 0% of the time, Pallas kernels for 0%

profile of v9, /device:TPU:2, one launch (start us, length us, event | category | flops | bytes accessed | tf_op | source)
XLA Modules:
  0.0 333.2 jit_solution(16675811357016700341)
XLA Ops:
  0.7 0.9 copy.113
  3.4 2.4 scatter_custom_fusion
  6.4 5.4 %gather_fusion = bf16[768,3584]{1,0:T(8,128)(2,1)} fusion(bf16[128,3584]{1,0:T(8,128)(2,1)S(1)} %broadcast_select_fusion, s32[1024]{0:T(1024)S(1)} %pad_clamp_fusion), kind=kCustom, calls=%fused_computation | custom fusion | bytes 11013120 | tf_op jit(solution)/shard_map/gather | solution.py:30
  11.9 11.4 %reshape.128 = bf16[128,3,2,3584]{3,2,1,0:T(2,128)(2,1)} reshape(bf16[768,3584]{1,0:T(8,128)(2,1)} %gather_fusion) | data formatting | bytes 11010048 | tf_op jit(solution)/shard_map/gather | solution.py:30
  23.3 140.4 %all_to_all.10 = bf16[128,3,2,3584]{3,2,1,0:T(2,128)(2,1)} all-to-all(bf16[128,3,2,3584]{3,2,1,0:T(2,128)(2,1)} %reshape.128), channel_id=1, replica_groups=mesh['expert'=128,'hid'=2] {'expert'}, dimensions={0} | all-to-all | bytes 11010048 | tf_op jit(solution)/shard_map/all_to_all | solution.py:31
  163.7 9.4 %collective-permute-done = bf16[128,3,2,3584]{3,2,1,0:T(2,128)(2,1)} collective-permute-done((bf16[128,3,2,3584]{3,2,1,0:T(2,128)(2,1)}, bf16[128,3,2,3584]{3,2,1,0:T(2,128)(2,1)}, u32[]{:S(2)}, u32[]{:S(2)}) %collective-permute-start) | collective-permute-done | bytes 5505056 | tf_op jit(solution)/shard_map/ppermute | solution.py:33
  173.1 29.7 %fusion.1 = (bf16[1,128,3,2,3584]{4,3,2,1,0:T(2,128)(2,1)S(1)}, bf16[1,128,3,2,3584]{4,3,2,1,0:T(2,128)(2,1)S(1)}) fusion(s32[]{:T(128)S(6)} %select_n.141, bf16[1,128,3,2,3584]{4,3,2,1,0:T(2,128)(2,1)} %bitcast.5, bf16[1,128,3,2,3584]{4,3,2,1,0:T(2,128)(2,1)} %bitcast.6, s32[]{:T(128)S(6)} %select_n.140), kind=kLoop, calls=%fused_computation.13 | loop fusion | flops 5505024 | bytes 22020104 | tf_op jit(solution)/shard_map/stack | solution.py:35
  202.8 3.0 fusion.3
  205.8 3.0 fusion.5
  208.8 3.4 %multiply_reduce_fusion = (f32[128,3,2]{0,2,1:T(2,128)S(1)}, f32[128,3,2,512]{3,0,2,1:T(8,128)S(1)}) fusion(f32[128,3,2,512]{3,0,2,1:T(8,128)S(1)} %fusion.5, f32[128,3,2,512]{3,0,2,1:T(8,128)S(1)} %fusion.3, bf16[1,512,3584]{2,1,0:T(8,128)(2,1)S(1)} %copy-done.6, bf16[1,128,3,2,3584]{4,3,2,1,0:T(2,128)(2,1)S(1)} %get-tuple-element.21), kind=kOutput, calls=%fused_computation.34 | convolution fusion | flops 2821324032 | bytes 13896704 | tf_op jit(solution)/shard_map/ejqc,fc->ejqf/dot_general | solution.py:43
  212.2 3.5 %fusion.12 = f32[128,3,2,3584]{3,0,2,1:T(8,128)S(1)} fusion(bf16[1,3584,512]{2,1,0:T(8,128)(2,1)S(1)} %copy-done, f32[128,3,2,512]{3,0,2,1:T(8,128)S(1)} %fusion.3, f32[128,3,2,512]{3,0,2,1:T(8,128)S(1)} %get-tuple-element.35, f32[128,3,2,512]{3,0,2,1:T(8,128)S(1)} %fusion.5), kind=kOutput, calls=%fused_computation.27 | convolution fusion | flops 2822504448 | bytes 19398656 | tf_op jit(solution)/shard_map/ejqf,cf->ejqc/dot_general | solution.py:53
  215.7 7.1 %convolution_add_fusion = bf16[128,3,2,3584]{3,0,2,1:T(8,128)(2,1)} fusion(f32[128,3,2,3584]{3,0,2,1:T(8,128)S(1)} %fusion.12, bf16[1,3584,512]{2,1,0:T(8,128)(2,1)} %param.14, f32[128,3,2,512]{3,0,2,1:T(8,128)S(1)} %get-tuple-element.35, f32[128,3,2,512]{3,0,2,1:T(8,128)S(1)} %fusion.3), kind=kOutput, calls=%fused_computation.10 | convolution fusion | flops 2826436608 | bytes 23330816 | tf_op jit(solution)/shard_map/ejqf,cf->ejqc/dot_general | solution.py:55
  222.8 3.5 %dynamic-slice_convert_fusion = bf16[128,3,2,1792]{3,0,2,1:T(8,128)(2,1)} fusion(bf16[128,3,2,3584]{3,0,2,1:T(8,128)(2,1)} %convolution_add_fusion, s32[]{:T(128)S(6)} %select_n.143), kind=kLoop, calls=%fused_computation.23 | loop fusion | bytes 5505028 | tf_op jit(solution)/shard_map/convert_element_type | solution.py:59
  226.8 4.8 %collective-permute-done.2 = f32[128,3,2]{0,2,1:T(2,128)S(1)} collective-permute-done((f32[128,3,2]{0,2,1:T(2,128)S(1)}, f32[128,3,2]{0,2,1:T(2,128)S(1)}, u32[]{:S(2)}, u32[]{:S(2)}) %collective-permute-start.2) | collective-permute-done | bytes 3104 | tf_op jit(solution)/shard_map/ppermute | solution.py:64
  231.8 2.4 add_convert_fusion
  234.6 4.6 %copy.120 = bf16[128,3,2,1920]{3,2,1,0:T(2,128)(2,1)} copy(bf16[128,3,2,1920]{3,0,2,1:T(8,128)(2,1)S(1)} %fusion.18) | data formatting | bytes 5898240 | tf_op jit(solution)/shard_map/concatenate | solution.py:66
  239.2 8.0 %all-to-all-start.1 = ((bf16[128,3,2,1920]{3,2,1,0:T(2,128)(2,1)}), bf16[128,3,2,1920]{3,2,1,0:T(2,128)(2,1)S(1)}, u32[]{:S(2)}, u32[]{:S(2)}) async-start(bf16[128,3,2,1920]{3,2,1,0:T(2,128)(2,1)} %copy.120), calls=%async_computation.1 | async-start | bytes 5898240 | tf_op jit(solution)/shard_map/all_to_all | solution.py:67
  247.8 69.9 %all-to-all-done.1 = bf16[128,3,2,1920]{3,2,1,0:T(2,128)(2,1)S(1)} async-done(((bf16[128,3,2,1920]{3,2,1,0:T(2,128)(2,1)}), bf16[128,3,2,1920]{3,2,1,0:T(2,128)(2,1)S(1)}, u32[]{:S(2)}, u32[]{:S(2)}) %all-to-all-start.1) | async-done | bytes 2949152 | tf_op jit(solution)/shard_map/all_to_all | solution.py:67
  317.7 1.9 gather_fusion.1
  319.6 2.7 gather_fusion.2
  322.3 0.8 slice.140
  323.1 2.7 gather_fusion.3
  326.6 2.6 gather_fusion.4
  330.7 2.5 add_convert_fusion.1
  (59 shorter events, 6.3 us)
Async XLA Ops:
  0.6 5.7 %copy-start.3 = (bf16[128,3584]{1,0:T(8,128)(2,1)S(1)}, bf16[128,3584]{1,0:T(8,128)(2,1)}, u32[]{:S(2)}) copy-start(bf16[128,3584]{1,0:T(8,128)(2,1)} %param.10) | copy-start | bytes 2752516
  0.6 5.7 %copy-start.2 = (bf16[128,3584]{1,0:T(8,128)(2,1)S(1)}, bf16[128,3584]{1,0:T(8,128)(2,1)}, u32[]{:S(2)}) copy-start(bf16[128,3584]{1,0:T(8,128)(2,1)} %param.9) | copy-start | bytes 2752516
  163.7 9.4 %collective-permute-start = (bf16[128,3,2,3584]{3,2,1,0:T(2,128)(2,1)}, bf16[128,3,2,3584]{3,2,1,0:T(2,128)(2,1)}, u32[]{:S(2)}, u32[]{:S(2)}) collective-permute-start(bf16[128,3,2,3584]{3,2,1,0:T(2,128)(2,1)} %all_to_all.10), channel_id=1, source_target_pairs={{0,1},{1,0},{2,3},{3,2},{4,5},{5,4},{6,7},{7,6},{8,9},{9,8},{10,11... | collective-permute-start | bytes 16515080 | tf_op jit(solution)/shard_map/ppermute | solution.py:33
  173.1 29.7 %copy-start = (bf16[1,3584,512]{2,1,0:T(8,128)(2,1)S(1)}, bf16[1,3584,512]{2,1,0:T(8,128)(2,1)}, u32[]{:S(2)}) copy-start(bf16[1,3584,512]{2,1,0:T(8,128)(2,1)} %param.13) | copy-start | bytes 11010052
  202.8 3.0 copy-start.1
  205.8 3.0 copy-start.6
  226.3 5.5 %collective-permute-start.1 = (bf16[128,3,2,1792]{3,0,2,1:T(8,128)(2,1)}, bf16[128,3,2,1792]{3,0,2,1:T(8,128)(2,1)S(1)}, u32[]{:S(2)}, u32[]{:S(2)}) collective-permute-start(bf16[128,3,2,1792]{3,0,2,1:T(8,128)(2,1)} %dynamic-slice_convert_fusion), channel_id=1, source_target_pairs={{0,1},{1,0},{2,3},{3,2},{4,5},{5,4},{6,7},{7,6},{8,9},{9,8},{10,11... | collective-permute-start | bytes 8257544 | tf_op jit(solution)/shard_map/ppermute | solution.py:60
  226.5 5.2 %collective-permute-start.2 = (f32[128,3,2]{0,2,1:T(2,128)S(1)}, f32[128,3,2]{0,2,1:T(2,128)S(1)}, u32[]{:S(2)}, u32[]{:S(2)}) collective-permute-start(f32[128,3,2]{0,2,1:T(2,128)S(1)} %get-tuple-element.34), channel_id=1, source_target_pairs={{0,1},{1,0},{2,3},{3,2},{4,5},{5,4},{6,7},{7,6},{8,9},{9,8},{10,11... | collective-permute-start | bytes 9224 | tf_op jit(solution)/shard_map/ppermute | solution.py:64
  239.2 8.5 %copy-start.5 = (f32[128,4]{0,1:T(4,128)S(1)}, f32[128,4]{0,1:T(4,128)}, u32[]{:S(2)}) copy-start(f32[128,4]{0,1:T(4,128)} %param.12) | copy-start | bytes 6148
  239.2 8.6 %copy-start.4 = (s32[128,4]{0,1:T(4,128)S(1)}, s32[128,4]{0,1:T(4,128)}, u32[]{:S(2)}) copy-start(s32[128,4]{0,1:T(4,128)} %param.11) | copy-start | bytes 6148
  239.2 78.5 %all-to-all-start.1 = ((bf16[128,3,2,1920]{3,2,1,0:T(2,128)(2,1)}), bf16[128,3,2,1920]{3,2,1,0:T(2,128)(2,1)S(1)}, u32[]{:S(2)}, u32[]{:S(2)}) async-start(bf16[128,3,2,1920]{3,2,1,0:T(2,128)(2,1)} %copy.120), calls=%async_computation.1 | async-start | bytes 5898240 | tf_op jit(solution)/shard_map/all_to_all | solution.py:67

commit v10 on v7

--- a/solution.py
+++ b/solution.py
@@ -56,13 +56,12 @@
     give_half = lax.dynamic_slice_in_dim(
         grad_part, (1 - hid_idx) * half_width, half_width, axis=3
     ).astype(jnp.bfloat16)
-    got_half = lax.ppermute(give_half, "hid", swap)
-    grad_share = (
-        own_half.astype(jnp.bfloat16).astype(jnp.float32) + got_half.astype(jnp.float32)
+    score_block = jnp.zeros(quad + (128,), jnp.float32).at[..., 0].set(score_part)
+    give = jnp.concatenate([give_half, score_block.astype(jnp.bfloat16)], axis=3)
+    got = lax.ppermute(give, "hid", swap)
+    back_send = (
+        jnp.concatenate([own_half, score_block], axis=3) + got.astype(jnp.float32)
     ).astype(jnp.bfloat16)
-    score_full = (score_part + lax.ppermute(score_part, "hid", swap)).astype(jnp.bfloat16)
-    score_cols = jnp.zeros(quad + (128,), jnp.bfloat16).at[..., 0].set(score_full)
-    back_send = jnp.concatenate([grad_share, score_cols], axis=3)
     back = lax.all_to_all(back_send, "expert", split_axis=0, concat_axis=0, tiled=True)
     route_slot = slot_index.reshape(tok_rows, top_count)
     token_grad = jnp.zeros((tok_rows, half_width), jnp.float32)

time: 315 us -> 315 us (level)
    convert_element_type x0 -> x1, local copies, waits for them, and re-layouts: none -> 4.63 us  [body(): back_send = (jnp.concatenate([own_half, score_block], axis=3) + got.astyp...]
    concatenate x1 -> x0, local copies, waits for them, and re-layouts: 4.63 us -> none  [body(): back_send = jnp.concatenate([grad_share, score_cols], axis=3)]
  transfers between devices with their start and end apart: 4 -> 3, of which waited for: 3 -> 3; matrix products, arithmetic and copies ran while one was open for 0% -> 1% of each run, Pallas kernels for 0% -> 0%
where the time goes in v10:
time: 315 us; the launch traced here: 314 us
  blocking collectives  140 us (44%)
  waiting for transfers between devices  81.4 us (26%)
  local copies, waits for them, and re-layouts  45 us (14%)
  matrix products  19.1 us (6%)
  other arithmetic  18.3 us (6%)
  starting transfers between devices  8.46 us (3%)
    all_to_all x1, blocking collectives, body(): lax.all_to_all(send, 'expert', split_axis=0, concat_axis=0, tiled=True)  140 us
    all_to_all x1, waiting for transfers between devices, body(): lax.all_to_all(back_send, 'expert', split_axis=0, concat_axis=0, tiled=True)  69.9 us
    gather x2, local copies, waits for them, and re-layouts, body(): send = source[slot_token.reshape(quad)]  16.9 us
    select_n x1, other arithmetic, body(): rows_x = jnp.where(first, recv, other)  11 us
    gather x4, local copies, waits for them, and re-layouts, body(): row = back[route_ids[:, k], route_slot[:, k] // 2, route_slot[:, k] % 2]  9.84 us
    ppermute x1, waiting for transfers between devices, body(): other = lax.ppermute(recv, 'hid', swap)  9.37 us
    all_to_all x1, starting transfers between devices, body(): lax.all_to_all(back_send, 'expert', split_axis=0, concat_axis=0, tiled=True)  7.98 us
  transfers between devices with their start and end apart: 3, of which 3 were waited for; matrix products, arithmetic and copies ran while one was open for 1% of the time, Pallas kernels for 0%

profile of v10, /device:TPU:2, one launch (start us, length us, event | category | flops | bytes accessed | tf_op | source)
XLA Modules:
  0.0 313.7 jit_solution(2803378352378509236)
XLA Ops:
  0.6 0.9 copy.114
  3.4 2.4 scatter_custom_fusion
  6.4 5.5 %gather_fusion = bf16[768,3584]{1,0:T(8,128)(2,1)} fusion(bf16[128,3584]{1,0:T(8,128)(2,1)S(1)} %broadcast_select_fusion.2, s32[1024]{0:T(1024)S(1)} %pad_clamp_fusion), kind=kCustom, calls=%fused_computation | custom fusion | bytes 11013120 | tf_op jit(solution)/shard_map/gather | solution.py:30
  11.9 11.4 %reshape.128 = bf16[128,3,2,3584]{3,2,1,0:T(2,128)(2,1)} reshape(bf16[768,3584]{1,0:T(8,128)(2,1)} %gather_fusion) | data formatting | bytes 11010048 | tf_op jit(solution)/shard_map/gather | solution.py:30
  23.3 140.4 %all_to_all.10 = bf16[128,3,2,3584]{3,2,1,0:T(2,128)(2,1)} all-to-all(bf16[128,3,2,3584]{3,2,1,0:T(2,128)(2,1)} %reshape.128), channel_id=1, replica_groups=mesh['expert'=128,'hid'=2] {'expert'}, dimensions={0} | all-to-all | bytes 11010048 | tf_op jit(solution)/shard_map/all_to_all | solution.py:31
  163.7 9.4 %collective-permute-done = bf16[128,3,2,3584]{3,2,1,0:T(2,128)(2,1)} collective-permute-done((bf16[128,3,2,3584]{3,2,1,0:T(2,128)(2,1)}, bf16[128,3,2,3584]{3,2,1,0:T(2,128)(2,1)}, u32[]{:S(2)}, u32[]{:S(2)}) %collective-permute-start) | collective-permute-done | bytes 5505056 | tf_op jit(solution)/shard_map/ppermute | solution.py:33
  173.1 11.0 %broadcast_select_fusion = (bf16[128,3,2,3584]{3,2,1,0:T(2,128)(2,1)S(1)}, bf16[128,3,2,3584]{3,2,1,0:T(2,128)(2,1)S(1)}) fusion(bf16[128,3,2,3584]{3,2,1,0:T(2,128)(2,1)} %all_to_all.10, bf16[128,3,2,3584]{3,2,1,0:T(2,128)(2,1)} %collective-permute-done, pred[]{:T(512)S(6)} %eq.34), kind=kLoop, calls=%fused_computation.6 | loop fusion | flops 5505024 | bytes 22020096 | tf_op jit(solution)/shard_map/jit(_where)/select_n | solution.py:35
  184.2 3.0 fusion.3
  187.2 3.0 fusion.5
  190.2 3.3 %multiply_reduce_fusion = (f32[128,3,2]{0,2,1:T(2,128)S(1)}, f32[128,3,2,512]{3,0,2,1:T(8,128)S(1)}) fusion(f32[128,3,2,512]{3,0,2,1:T(8,128)S(1)} %fusion.5, f32[128,3,2,512]{3,0,2,1:T(8,128)S(1)} %fusion.3, bf16[1,512,3584]{2,1,0:T(8,128)(2,1)S(1)} %copy-done.6, bf16[128,3,2,3584]{3,2,1,0:T(2,128)(2,1)S(1)} %get-tuple-element.21), kind=kOutput, calls=%fused_computation.25 | convolution fusion | flops 2821324032 | bytes 13896704 | tf_op jit(solution)/shard_map/ejqc,fc->ejqf/dot_general | solution.py:42
  193.5 3.5 %fusion.7 = f32[128,3,2,3584]{3,0,2,1:T(8,128)S(1)} fusion(bf16[1,3584,512]{2,1,0:T(8,128)(2,1)S(1)} %copy-done, f32[128,3,2,512]{3,0,2,1:T(8,128)S(1)} %fusion.3, f32[128,3,2,512]{3,0,2,1:T(8,128)S(1)} %get-tuple-element.35, f32[128,3,2,512]{3,0,2,1:T(8,128)S(1)} %fusion.5), kind=kOutput, calls=%fused_computation.18 | convolution fusion | flops 2822504448 | bytes 19398656 | tf_op jit(solution)/shard_map/ejqf,cf->ejqc/dot_general | solution.py:52
  197.0 6.3 %convolution_add_fusion = f32[128,3,2,3584]{3,0,2,1:T(8,128)} fusion(f32[128,3,2,3584]{3,0,2,1:T(8,128)S(1)} %fusion.7, bf16[1,3584,512]{2,1,0:T(8,128)(2,1)S(1)} %copy-done.1, f32[128,3,2,512]{3,0,2,1:T(8,128)S(1)} %get-tuple-element.35, f32[128,3,2,512]{3,0,2,1:T(8,128)S(1)} %fusion.3), kind=kOutput, calls=%fused_computation.8 | convolution fusion | flops 2823684096 | bytes 28835840 | tf_op jit(solution)/shard_map/ejqf,cf->ejqc/dot_general | solution.py:54
  203.5 2.8 dynamic-slice_convert_fusion
  207.2 3.1 %constant_dynamic-slice_fusion = f32[128,3,2,1792]{3,0,2,1:T(8,128)S(1)} fusion(f32[128,3,2,3584]{3,0,2,1:T(8,128)} %convolution_add_fusion, s32[]{:T(128)S(6)} %select_n.148), kind=kLoop, calls=%fused_computation.125 | loop fusion | bytes 11010052 | tf_op jit(solution)/shard_map/dynamic_slice | solution.py:55
  210.4 2.2 collective-permute-done.1
  212.5 2.5 fusion
  215.0 4.6 %copy.122 = bf16[128,3,2,1920]{3,2,1,0:T(2,128)(2,1)} copy(bf16[128,3,2,1920]{3,0,2,1:T(8,128)(2,1)S(1)} %fusion) | data formatting | bytes 5898240 | tf_op jit(solution)/shard_map/convert_element_type | solution.py:64
  219.7 8.0 %all-to-all-start.1 = ((bf16[128,3,2,1920]{3,2,1,0:T(2,128)(2,1)}), bf16[128,3,2,1920]{3,2,1,0:T(2,128)(2,1)S(1)}, u32[]{:S(2)}, u32[]{:S(2)}) async-start(bf16[128,3,2,1920]{3,2,1,0:T(2,128)(2,1)} %copy.122), calls=%async_computation.1 | async-start | bytes 5898240 | tf_op jit(solution)/shard_map/all_to_all | solution.py:65
  228.3 69.9 %all-to-all-done.1 = bf16[128,3,2,1920]{3,2,1,0:T(2,128)(2,1)S(1)} async-done(((bf16[128,3,2,1920]{3,2,1,0:T(2,128)(2,1)}), bf16[128,3,2,1920]{3,2,1,0:T(2,128)(2,1)S(1)}, u32[]{:S(2)}, u32[]{:S(2)}) %all-to-all-start.1) | async-done | bytes 2949152 | tf_op jit(solution)/shard_map/all_to_all | solution.py:65
  298.1 1.9 gather_fusion.1
  300.1 2.7 gather_fusion.2
  303.6 2.7 gather_fusion.3
  307.1 2.6 gather_fusion.4
  311.2 2.5 add_convert_fusion
  (59 shorter events, 7.1 us)
Async XLA Ops:
  0.6 5.7 %copy-start.3 = (bf16[128,3584]{1,0:T(8,128)(2,1)S(1)}, bf16[128,3584]{1,0:T(8,128)(2,1)}, u32[]{:S(2)}) copy-start(bf16[128,3584]{1,0:T(8,128)(2,1)} %param.10) | copy-start | bytes 2752516
  0.6 5.7 %copy-start.2 = (bf16[128,3584]{1,0:T(8,128)(2,1)S(1)}, bf16[128,3584]{1,0:T(8,128)(2,1)}, u32[]{:S(2)}) copy-start(bf16[128,3584]{1,0:T(8,128)(2,1)} %param.9) | copy-start | bytes 2752516
  163.7 9.4 %collective-permute-start = (bf16[128,3,2,3584]{3,2,1,0:T(2,128)(2,1)}, bf16[128,3,2,3584]{3,2,1,0:T(2,128)(2,1)}, u32[]{:S(2)}, u32[]{:S(2)}) collective-permute-start(bf16[128,3,2,3584]{3,2,1,0:T(2,128)(2,1)} %all_to_all.10), channel_id=1, source_target_pairs={{0,1},{1,0},{2,3},{3,2},{4,5},{5,4},{6,7},{7,6},{8,9},{9,8},{10,11... | collective-permute-start | bytes 16515080 | tf_op jit(solution)/shard_map/ppermute | solution.py:33
  163.7 20.4 %copy-start = (bf16[1,3584,512]{2,1,0:T(8,128)(2,1)S(1)}, bf16[1,3584,512]{2,1,0:T(8,128)(2,1)}, u32[]{:S(2)}) copy-start(bf16[1,3584,512]{2,1,0:T(8,128)(2,1)} %param.13) | copy-start | bytes 11010052
  184.2 3.0 copy-start.1
  187.2 3.0 copy-start.6
  206.7 5.8 %collective-permute-start.1 = (bf16[128,3,2,1920]{3,0,2,1:T(8,128)(2,1)S(1)}, bf16[128,3,2,1920]{3,0,2,1:T(8,128)(2,1)}, u32[]{:S(2)}, u32[]{:S(2)}) collective-permute-start(bf16[128,3,2,1920]{3,0,2,1:T(8,128)(2,1)S(1)} %pad_maximum_fusion), channel_id=1, source_target_pairs={{0,1},{1,0},{2,3},{3,2},{4,5},{5,4},{6,7},{7,6},{8,9},{9,8},{10,11... | collective-permute-start | bytes 8847368 | tf_op jit(solution)/shard_map/ppermute | solution.py:61
  219.7 8.5 %copy-start.5 = (f32[128,4]{0,1:T(4,128)S(1)}, f32[128,4]{0,1:T(4,128)}, u32[]{:S(2)}) copy-start(f32[128,4]{0,1:T(4,128)} %param.12) | copy-start | bytes 6148
  219.7 8.6 %copy-start.4 = (s32[128,4]{0,1:T(4,128)S(1)}, s32[128,4]{0,1:T(4,128)}, u32[]{:S(2)}) copy-start(s32[128,4]{0,1:T(4,128)} %param.11) | copy-start | bytes 6148
  219.7 78.5 %all-to-all-start.1 = ((bf16[128,3,2,1920]{3,2,1,0:T(2,128)(2,1)}), bf16[128,3,2,1920]{3,2,1,0:T(2,128)(2,1)S(1)}, u32[]{:S(2)}, u32[]{:S(2)}) async-start(bf16[128,3,2,1920]{3,2,1,0:T(2,128)(2,1)} %copy.122), calls=%async_computation.1 | async-start | bytes 5898240 | tf_op jit(solution)/shard_map/all_to_all | solution.py:65
